TPU v7x, 256 devices: a whole 4x4x8 slice. The times are simulated.
256 devices in a mesh: ta: 8 (over x_lo, y), gx: 4 (over x_hi, core), yz: 8 (over z).
Axes of the slice: x: 4 (x_hi: 2, x_lo: 2; x = x_hi * 2 + x_lo), y: 4, z: 8, core: 2. Of those that a mesh axis runs over, the one named last changes fastest.
Arguments:
- vectors: bfloat16 [2, 3, 32, 64, 256, 128], P(None, None, 'gx', 'yz', 'ta'), parts along dimension 4, may hold values from -6 to 6
- gauge_x: float32 [2, 3, 3, 32, 64, 256], P(None, None, None, 'gx', 'yz', 'ta'), parts along dimension 5, may hold values from -6 to 6
- gauge_y: float32 [2, 3, 3, 32, 64, 256], P(None, None, None, 'gx', 'yz', 'ta'), parts along dimension 5, may hold values from -6 to 6
Outputs:
- elementals: float32 [16, 2, 128, 128], P('ta'), parts along dimension 0
There are 8 independent parts, one for each index of `ta`. A program takes and returns all parts, laid end to end along the dimension named above; each array names one. Nothing has to cross between parts.
All inputs are finite; a program needn't handle non-finite values.
Results may differ from a plain program's by a relative error of at most 0.0029.
Values may be sent and summed in bfloat16 or wider, within the bound.
No kernel may reach another device: no remote copies, remote signals or barrier semaphores. Data moves between devices by JAX's collectives and lax.ppermute only.
A program may use at most 64 MiB of HBM per device.

v0:
```python
import math

import jax
import jax.numpy as jnp
from jax import lax
from jax.sharding import PartitionSpec as P


def shifted(value, axis, steps):
    count = lax.axis_size(axis)
    pairs = [(source, (source + steps) % count) for source in range(count)]
    return lax.ppermute(value, axis, pairs)


def colour_apply(gauge, source_vectors):
    real_parts = []
    imag_parts = []
    for colour in range(3):
        real_running = jnp.zeros(source_vectors.shape[2:], jnp.float32)
        imaginary_running = jnp.zeros(source_vectors.shape[2:], jnp.float32)
        for inner_product in range(3):
            left_real = gauge[0, colour, inner_product][..., None]
            left_imaginary = gauge[1, colour, inner_product][..., None]
            right_real = source_vectors[0, inner_product].astype(jnp.float32)
            right_imaginary = source_vectors[1, inner_product].astype(jnp.float32)
            real_running = real_running + left_real * right_real - left_imaginary * right_imaginary
            imaginary_running = (
                imaginary_running + left_real * right_imaginary + left_imaginary * right_real
            )
        real_parts.append(real_running)
        imag_parts.append(imaginary_running)
    return jnp.stack([jnp.stack(real_parts), jnp.stack(imag_parts)]).astype(jnp.bfloat16)


def right_block(image):
    nvecs = image.shape[-1]
    real_rows = image[0].reshape(-1, nvecs)
    imag_rows = image[1].reshape(-1, nvecs)
    first = jnp.concatenate([real_rows, imag_rows], 0)
    second = jnp.concatenate([imag_rows, -real_rows], 0)
    return (first, second)


def contract(left_cols, right_cols):
    return lax.dot_general(
        left_cols, right_cols, (((0,), (0,)), ((), ())), preferred_element_type=jnp.float32
    )


def local(vectors, gauge_x, gauge_y):
    nvecs = vectors.shape[-1]
    from_next_x = shifted(vectors[:, :, :1], "gx", -1)
    shifted_x = jnp.concatenate([vectors[:, :, 1:], from_next_x], 2)
    from_next_y = shifted(vectors[:, :, :, :1], "yz", -1)
    shifted_y = jnp.concatenate([vectors[:, :, :, 1:], from_next_y], 3)
    image_x = colour_apply(gauge_x, shifted_x)
    image_y = colour_apply(gauge_y, shifted_y)
    left_rows = vectors.reshape(-1, nvecs)
    blocks = right_block(image_x) + right_block(image_y)
    summed = lax.psum(
        jnp.concatenate([contract(left_rows, member) for member in blocks], 1), ("gx", "yz")
    )
    sites_total = (
        vectors.shape[2]
        * lax.axis_size("gx")
        * vectors.shape[3]
        * lax.axis_size("yz")
        * vectors.shape[4]
    )
    scaling = 1.0 / math.sqrt(3.0 * sites_total)
    return (summed * scaling).reshape(nvecs, 2, 2, nvecs).transpose(1, 2, 0, 3)


def solution(mesh):
    placed = (
        P(None, None, "gx", "yz", "ta", None),
        P(None, None, None, "gx", "yz", "ta"),
        P(None, None, None, "gx", "yz", "ta"),
    )
    return jax.shard_map(
        local, mesh=mesh, in_specs=placed, out_specs=P("ta", None, None, None), check_vma=False
    )
```

profile of v0, /device:TPU:1, one launch (start us, length us, event | category | flops | bytes accessed | tf_op | source)
XLA Modules:
  0.0 311.7 jit_solution(16234775033811610859)
XLA Ops:
  6.5 1.0 slice.186
  7.6 3.3 %collective-permute-start = (bf16[2,3,1,8,32,128]{5,4,3,2,1,0:T(8,128)(2,1)S(1)}, bf16[2,3,1,8,32,128]{5,4,3,2,1,0:T(8,128)(2,1)S(1)}, u32[]{:S(2)}, u32[]{:S(2)}) collective-permute-start(bf16[2,3,1,8,32,128]{5,4,3,2,1,0:T(8,128)(2,1)S(1)} %slice.186), channel_id=1, source_target_pairs={{0,24},{8,0},{16,8},{24,16},{1,25},{9,1},{17,9},{25,17},{2,26},{10... | collective-permute-start | bytes 1179656 | tf_op jit(solution)/shard_map/ppermute | solution.py:12
  10.9 1.0 slice.212
  11.9 4.1 %collective-permute-start.1 = (bf16[2,3,8,1,32,128]{5,4,3,2,1,0:T(8,128)(2,1)S(1)}, bf16[2,3,8,1,32,128]{5,4,3,2,1,0:T(8,128)(2,1)S(1)}, u32[]{:S(2)}, u32[]{:S(2)}) collective-permute-start(bf16[2,3,8,1,32,128]{5,4,3,2,1,0:T(8,128)(2,1)S(1)} %slice.212), channel_id=1, source_target_pairs={{0,7},{1,0},{2,1},{3,2},{4,3},{5,4},{6,5},{7,6},{8,15},{9,8},{10,9... | collective-permute-start | bytes 1179656 | tf_op jit(solution)/shard_map/ppermute | solution.py:12
  16.0 0.7 slice.211
  16.7 0.4 copy-done.1
  17.3 0.8 slice-done
  18.2 2.1 fusion.51
  20.2 1.9 fusion.33
  22.2 3.9 %fusion.57 = (bf16[1,8,8,32,128]{4,3,2,1,0:T(8,128)(2,1)S(1)}, bf16[1,8,8,32,128]{4,3,2,1,0:T(8,128)(2,1)S(1)}, bf16[1,8,8,32,128]{4,3,2,1,0:T(8,128)(2,1)S(1)}, bf16[1,8,8,32,128]{4,3,2,1,0:T(8,128)(2,1)S(1)}) fusion(bf16[1,8,8,32,128]{4,3,2,1,0:T(8,128)(2,1)S(1)} %get-tuple-element.11, bf16[1,8,8,32,128]{4,3,2,1,0:T(8,128)(2,1)S(1)} %get-tuple-element.10, ...), kind=kLoop, calls=%fused_computation.145 | loop fusion | flops 14155776 | bytes 5341184 | tf_op jit(solution)/shard_map/convert.26
  26.1 0.3 pad_maximum_fusion
  26.5 0.3 bitcast_negate_fusion.1
  26.8 1.0 fusion.25
  27.8 1.0 fusion.22
  28.9 2.0 fusion.87
  30.9 1.9 fusion.69
  32.8 3.9 %fusion.93 = (bf16[1,8,8,32,128]{4,3,2,1,0:T(8,128)(2,1)S(1)}, bf16[1,8,8,32,128]{4,3,2,1,0:T(8,128)(2,1)S(1)}, bf16[1,8,8,32,128]{4,3,2,1,0:T(8,128)(2,1)S(1)}, bf16[1,8,8,32,128]{4,3,2,1,0:T(8,128)(2,1)S(1)}) fusion(bf16[1,8,8,32,128]{4,3,2,1,0:T(8,128)(2,1)S(1)} %get-tuple-element.18, bf16[1,8,8,32,128]{4,3,2,1,0:T(8,128)(2,1)S(1)} %get-tuple-element.17, ...), kind=kLoop, calls=%fused_computation.181 | loop fusion | flops 14155776 | bytes 5341184 | tf_op jit(solution)/shard_map/convert.16
  36.8 0.3 pad_maximum_fusion.2
  37.4 1.0 fusion.19
  38.5 1.1 fusion.16
  39.5 0.7 pad_maximum_fusion.6
  40.3 262.8 %all-reduce.2.cloned.1.call-done = f32[128,512]{0,1:T(8,128)} async-done(((f32[128,512]{0,1:T(8,128)}), f32[128,512]{0,1:T(8,128)}) %all-reduce.2.cloned.1.call-update) | async-done | bytes 262160 | tf_op jit(solution)/shard_map/psum | solution.py:60
  303.1 1.0 broadcast_multiply_fusion
  304.0 0.8 copy.4
  (13 shorter events, 0.6 us)
Async XLA Ops:
  6.5 296.5 %all-reduce.2.cloned.1.call-start = ((), (), s32[]{:S(2)}) async-start(), calls=%async_computation | async-start | bytes 524288 | tf_op jit(solution)/shard_map/psum | solution.py:60
  7.6 8.5 %copy-start = (bf16[2,3,8,8,32,128]{5,4,3,2,1,0:T(8,128)(2,1)S(1)}, bf16[2,3,8,8,32,128]{5,4,3,2,1,0:T(8,128)(2,1)}, u32[]{:S(2)}) copy-start(bf16[2,3,8,8,32,128]{5,4,3,2,1,0:T(8,128)(2,1)} %param.3) | copy-start | bytes 9437188
  7.6 9.8 %collective-permute-start = (bf16[2,3,1,8,32,128]{5,4,3,2,1,0:T(8,128)(2,1)S(1)}, bf16[2,3,1,8,32,128]{5,4,3,2,1,0:T(8,128)(2,1)S(1)}, u32[]{:S(2)}, u32[]{:S(2)}) collective-permute-start(bf16[2,3,1,8,32,128]{5,4,3,2,1,0:T(8,128)(2,1)S(1)} %slice.186), channel_id=1, source_target_pairs={{0,24},{8,0},{16,8},{24,16},{1,25},{9,1},{17,9},{25,17},{2,26},{10... | collective-permute-start | bytes 1179656 | tf_op jit(solution)/shard_map/ppermute | solution.py:12
  11.9 16.9 %collective-permute-start.1 = (bf16[2,3,8,1,32,128]{5,4,3,2,1,0:T(8,128)(2,1)S(1)}, bf16[2,3,8,1,32,128]{5,4,3,2,1,0:T(8,128)(2,1)S(1)}, u32[]{:S(2)}, u32[]{:S(2)}) collective-permute-start(bf16[2,3,8,1,32,128]{5,4,3,2,1,0:T(8,128)(2,1)S(1)} %slice.212), channel_id=1, source_target_pairs={{0,7},{1,0},{2,1},{3,2},{4,3},{5,4},{6,5},{7,6},{8,15},{9,8},{10,9... | collective-permute-start | bytes 1179656 | tf_op jit(solution)/shard_map/ppermute | solution.py:12
  16.0 1.1 copy-start.1
  16.0 1.2 copy-start.2
  16.0 2.1 slice-start
Sparse Core Ops, SparseCore 0:
  40.4 262.6 all-reduce.1
where the time goes:
time: 315 us; the launch traced here: 312 us
  waiting for transfers between devices  263 us (83%)
  other arithmetic  18.8 us (6%)
  between operations  13.6 us (4%)
  starting transfers between devices  7.42 us (2%)
  local copies, waits for them, and re-layouts  5 us (2%)
  matrix products  4.17 us (1%)
    psum x1, waiting for transfers between devices, local(): lax.psum(jnp.concatenate([contract(left_rows, member) for member in block...  263 us
    another operation x6, other arithmetic  15.8 us
    ppermute x2, starting transfers between devices, shifted(): return lax.ppermute(value, axis, pairs)  7.42 us
  transfers between devices with their start and end apart: 3, of which 1 were waited for; matrix products, arithmetic and copies ran while one was open for 4% of the time, Pallas kernels for 0%

commit v1 on v0

--- a/solution.py
+++ b/solution.py
@@ -47,6 +47,30 @@
     )
 
 
+STEPS = [("gx", 1), ("gx", 2), ("yz", 1), ("yz", 2), ("yz", 4)]
+
+def reduce_partials(x):
+    shape = x.shape
+    flat = x.reshape(-1)
+    bits = []
+    for axis, bit in STEPS:
+        size = lax.axis_size(axis)
+        high = (lax.axis_index(axis) & bit) != 0
+        half = flat.shape[0] // 2
+        lower, upper = flat[:half], flat[half:]
+        keep = jnp.where(high, upper, lower)
+        send = jnp.where(high, lower, upper)
+        pairs = [(j, j ^ bit) for j in range(size)]
+        flat = keep + lax.ppermute(send, axis, pairs)
+        bits.append(high)
+    for (axis, bit), high in reversed(list(zip(STEPS, bits))):
+        size = lax.axis_size(axis)
+        pairs = [(j, j ^ bit) for j in range(size)]
+        other = lax.ppermute(flat, axis, pairs)
+        flat = jnp.where(high, jnp.concatenate([other, flat]), jnp.concatenate([flat, other]))
+    return flat.reshape(shape)
+
+
 def local(vectors, gauge_x, gauge_y):
     nvecs = vectors.shape[-1]
     from_next_x = shifted(vectors[:, :, :1], "gx", -1)
@@ -57,9 +81,7 @@
     image_y = colour_apply(gauge_y, shifted_y)
     left_rows = vectors.reshape(-1, nvecs)
     blocks = right_block(image_x) + right_block(image_y)
-    summed = lax.psum(
-        jnp.concatenate([contract(left_rows, member) for member in blocks], 1), ("gx", "yz")
-    )
+    summed = reduce_partials(jnp.concatenate([contract(left_rows, member) for member in blocks], 1))
     sites_total = (
         vectors.shape[2]
         * lax.axis_size("gx")

time: 315 us -> 95.7 us (0.30)
  waiting for transfers between devices: 263 us -> 31.5 us
  starting transfers between devices: 7.42 us -> 24.9 us
  between operations: 13.6 us -> 0.28 us
  local copies, waits for them, and re-layouts: 5 us -> 13.1 us
    psum x1 -> x0, waiting for transfers between devices: 263 us -> none  [local(): lax.psum(jnp.concatenate([contract(left_rows, member) for member in block...]
    ppermute x0 -> x10, waiting for transfers between devices: none -> 31.5 us  [the longest x5 16.1 us: reduce_partials(): flat = keep + lax.ppermute(send, axis, pairs)]
    ppermute x0 -> x10, starting transfers between devices: none -> 17.5 us  [the longest x5 12.4 us: reduce_partials(): other = lax.ppermute(flat, axis, pairs)]
    slice x2 -> x1, local copies, waits for them, and re-layouts: 0.84 us -> 4.17 us  [local(): shifted_x = jnp.concatenate([vectors[:, :, 1:], from_next_x], 2)]
    another operation x6, other arithmetic: 15.8 us -> 19.1 us
  transfers between devices with their start and end apart: 3 -> 12, of which waited for: 1 -> 10; matrix products, arithmetic and copies ran while one was open for 4% -> 24% of each run, Pallas kernels for 0% -> 0%
where the time goes in v1:
time: 95.7 us; the launch traced here: 95.1 us
  waiting for transfers between devices  31.5 us (33%)
  starting transfers between devices  24.9 us (26%)
  other arithmetic  20.9 us (22%)
  local copies, waits for them, and re-layouts  13.1 us (14%)
  matrix products  4.29 us (4%)
    another operation x6, other arithmetic  19.1 us
    ppermute x5, waiting for transfers between devices, reduce_partials(): flat = keep + lax.ppermute(send, axis, pairs)  16.1 us
    ppermute x5, waiting for transfers between devices, reduce_partials(): other = lax.ppermute(flat, axis, pairs)  15.4 us
    ppermute x5, starting transfers between devices, reduce_partials(): other = lax.ppermute(flat, axis, pairs)  12.4 us
    ppermute x2, starting transfers between devices, shifted(): return lax.ppermute(value, axis, pairs)  7.43 us
    ppermute x5, starting transfers between devices, reduce_partials(): flat = keep + lax.ppermute(send, axis, pairs)  5.06 us
    dot_general x4, matrix products, contract(): lax.dot_general(left_cols, right_cols, (((0,), (0,)), ((), ())), preferre...  4.29 us
    slice x1, local copies, waits for them, and re-layouts, local(): shifted_x = jnp.concatenate([vectors[:, :, 1:], from_next_x], 2)  4.17 us
  transfers between devices with their start and end apart: 12, of which 10 were waited for; matrix products, arithmetic and copies ran while one was open for 24% of the time, Pallas kernels for 0%

profile of v1, /device:TPU:1, one launch (start us, length us, event | category | flops | bytes accessed | tf_op | source)
XLA Modules:
  0.0 95.1 jit_solution(15254333048173354148)
XLA Ops:
  0.0 1.8 %slice.218 = bf16[2,3,1,8,32,128]{5,4,3,2,1,0:T(8,128)(2,1)} slice(bf16[2,3,8,8,32,128]{5,4,3,2,1,0:T(8,128)(2,1)} %param.3), slice={[0:2], [0:3], [0:1], [0:8], [0:32], [0:128]} | slice | bytes 786432 | tf_op jit(solution)/shard_map/slice | solution.py:76
  1.8 3.2 %collective-permute-start = (bf16[2,3,1,8,32,128]{5,4,3,2,1,0:T(8,128)(2,1)}, bf16[2,3,1,8,32,128]{5,4,3,2,1,0:T(8,128)(2,1)}, u32[]{:S(2)}, u32[]{:S(2)}) collective-permute-start(bf16[2,3,1,8,32,128]{5,4,3,2,1,0:T(8,128)(2,1)} %slice.218), channel_id=1, source_target_pairs={{0,24},{8,0},{16,8},{24,16},{1,25},{9,1},{17,9},{25,17},{2,26},{10... | collective-permute-start | bytes 1179656 | tf_op jit(solution)/shard_map/ppermute | solution.py:12
  6.1 4.2 %collective-permute-start.1 = (bf16[2,3,8,1,32,128]{5,4,3,2,1,0:T(8,128)(2,1)S(1)}, bf16[2,3,8,1,32,128]{5,4,3,2,1,0:T(8,128)(2,1)}, u32[]{:S(2)}, u32[]{:S(2)}) collective-permute-start(bf16[2,3,8,1,32,128]{5,4,3,2,1,0:T(8,128)(2,1)S(1)} %slice.244), channel_id=1, source_target_pairs={{0,7},{1,0},{2,1},{3,2},{4,3},{5,4},{6,5},{7,6},{8,15},{9,8},{10,9... | collective-permute-start | bytes 1179656 | tf_op jit(solution)/shard_map/ppermute | solution.py:12
  10.2 4.2 %slice.217 = bf16[2,3,7,8,32,128]{5,4,3,2,1,0:T(8,128)(2,1)} slice(bf16[2,3,8,8,32,128]{5,4,3,2,1,0:T(8,128)(2,1)} %param.3), slice={[0:2], [0:3], [1:8], [0:8], [0:32], [0:128]} | slice | bytes 5505024 | tf_op jit(solution)/shard_map/slice | solution.py:77
  14.4 2.3 %slice.243 = bf16[2,3,8,7,32,128]{5,4,3,2,1,0:T(8,128)(2,1)} slice(bf16[2,3,8,8,32,128]{5,4,3,2,1,0:T(8,128)(2,1)S(1)} %copy-done), slice={[0:2], [0:3], [0:8], [1:8], [0:32], [0:128]} | slice | bytes 5505024 | tf_op jit(solution)/shard_map/slice | solution.py:79
  18.9 4.1 %fusion.51 = (bf16[1,8,8,32,128]{4,3,2,1,0:T(8,128)(2,1)S(1)}, bf16[1,8,8,32,128]{4,3,2,1,0:T(8,128)(2,1)S(1)}, bf16[1,8,8,32,128]{4,3,2,1,0:T(8,128)(2,1)S(1)},...) fusion(f32[8,8,32]{2,1,0:T(8,128)S(1)} %get-tuple-element.41, ...), kind=kLoop, calls=%fused_computation.139 | loop fusion | flops 6291456 | bytes 6864896 | tf_op jit(solution)/shard_map/convert.25
  23.0 2.0 %fusion.33 = bf16[1,8,8,32,128]{4,3,2,1,0:T(8,128)(2,1)S(1)} fusion(bf16[1,8,8,32,128]{4,3,2,1,0:T(8,128)(2,1)S(1)} %get-tuple-element.11, bf16[1,8,8,32,128]{4,3,2,1,0:T(8,128)(2,1)S(1)} %get-tuple-element.10, bf16[1,8,8,32,128]{4,3,2,1,0:T(8,128)(2,1)S(1)} %get-tuple-element.9, bf16[1,8,8,32,128]{4,3,2,1,0:T(8,128)(2,1)S(1)} %get-tuple-element.8, ...), kind=kLoop, calls=%fused_computation.121 | loop fusion | flops 4718592 | bytes 3719168 | tf_op jit(solution)/shard_map/convert.29
  25.0 3.9 %fusion.57 = (bf16[1,8,8,32,128]{4,3,2,1,0:T(8,128)(2,1)S(1)}, bf16[1,8,8,32,128]{4,3,2,1,0:T(8,128)(2,1)S(1)}, bf16[1,8,8,32,128]{4,3,2,1,0:T(8,128)(2,1)S(1)}, bf16[1,8,8,32,128]{4,3,2,1,0:T(8,128)(2,1)S(1)}) fusion(bf16[1,8,8,32,128]{4,3,2,1,0:T(8,128)(2,1)S(1)} %get-tuple-element.11, bf16[1,8,8,32,128]{4,3,2,1,0:T(8,128)(2,1)S(1)} %get-tuple-element.10, ...), kind=kLoop, calls=%fused_computation.145 | loop fusion | flops 14155776 | bytes 5341184 | tf_op jit(solution)/shard_map/convert.26
  32.4 3.2 %fusion.87 = (bf16[1,8,8,32,128]{4,3,2,1,0:T(8,128)(2,1)S(1)}, bf16[1,8,8,32,128]{4,3,2,1,0:T(8,128)(2,1)S(1)}, bf16[1,8,8,32,128]{4,3,2,1,0:T(8,128)(2,1)S(1)},...) fusion(f32[8,8,32]{2,1,0:T(8,128)S(1)} %get-tuple-element.59, ...), kind=kLoop, calls=%fused_computation.175 | loop fusion | flops 6291456 | bytes 6864896 | tf_op jit(solution)/shard_map/convert.15
  35.6 2.0 %fusion.69 = bf16[1,8,8,32,128]{4,3,2,1,0:T(8,128)(2,1)S(1)} fusion(bf16[1,8,8,32,128]{4,3,2,1,0:T(8,128)(2,1)S(1)} %get-tuple-element.18, bf16[1,8,8,32,128]{4,3,2,1,0:T(8,128)(2,1)S(1)} %get-tuple-element.17, bf16[1,8,8,32,128]{4,3,2,1,0:T(8,128)(2,1)S(1)} %get-tuple-element.16, bf16[1,8,8,32,128]{4,3,2,1,0:T(8,128)(2,1)S(1)} %get-tuple-element.15, ...), kind=kLoop, calls=%fused_computation.157 | loop fusion | flops 4718592 | bytes 3719168 | tf_op jit(solution)/shard_map/convert.19
  37.6 3.9 %fusion.93 = (bf16[1,8,8,32,128]{4,3,2,1,0:T(8,128)(2,1)S(1)}, bf16[1,8,8,32,128]{4,3,2,1,0:T(8,128)(2,1)S(1)}, bf16[1,8,8,32,128]{4,3,2,1,0:T(8,128)(2,1)S(1)}, bf16[1,8,8,32,128]{4,3,2,1,0:T(8,128)(2,1)S(1)}) fusion(bf16[1,8,8,32,128]{4,3,2,1,0:T(8,128)(2,1)S(1)} %get-tuple-element.18, bf16[1,8,8,32,128]{4,3,2,1,0:T(8,128)(2,1)S(1)} %get-tuple-element.17, ...), kind=kLoop, calls=%fused_computation.181 | loop fusion | flops 14155776 | bytes 5341184 | tf_op jit(solution)/shard_map/convert.16
  44.7 2.7 %collective-permute-start.2 = (f32[32768]{0:T(1024)S(1)}, f32[32768]{0:T(1024)S(1)}, u32[]{:S(2)}, u32[]{:S(2)}) collective-permute-start(f32[32768]{0:T(1024)S(1)} %bitcast.166), channel_id=1, source_target_pairs={{0,8},{8,0},{16,24},{24,16},{1,9},{9,1},{17,25},{25,17},{2,10},{10... | collective-permute-start | bytes 393224 | tf_op jit(solution)/shard_map/ppermute | solution.py:64
  49.2 4.0 %collective-permute-done.3 = f32[16384]{0:T(1024)S(1)} collective-permute-done((f32[16384]{0:T(1024)S(1)}, f32[16384]{0:T(1024)S(1)}, u32[]{:S(2)}, u32[]{:S(2)}) %collective-permute-start.3) | collective-permute-done | bytes 65568 | tf_op jit(solution)/shard_map/ppermute | solution.py:64
  53.3 2.7 %collective-permute-done.4 = f32[8192]{0:T(1024)S(1)} collective-permute-done((f32[8192]{0:T(1024)S(1)}, f32[8192]{0:T(1024)S(1)}, u32[]{:S(2)}, u32[]{:S(2)}) %collective-permute-start.4) | collective-permute-done | bytes 32800 | tf_op jit(solution)/shard_map/ppermute | solution.py:64
  56.2 3.5 %collective-permute-done.5 = f32[4096]{0:T(1024)S(1)} collective-permute-done((f32[4096]{0:T(1024)S(1)}, f32[4096]{0:T(1024)S(1)}, u32[]{:S(2)}, u32[]{:S(2)}) %collective-permute-start.5) | collective-permute-done | bytes 16416 | tf_op jit(solution)/shard_map/ppermute | solution.py:64
  59.6 1.4 %collective-permute-start.6 = (f32[2048]{0:T(1024)S(1)}, f32[2048]{0:T(1024)S(1)}, u32[]{:S(2)}, u32[]{:S(2)}) collective-permute-start(f32[2048]{0:T(1024)S(1)} %slice_select_fusion.5), channel_id=1, source_target_pairs={{0,4},{1,5},{2,6},{3,7},{4,0},{5,1},{6,2},{7,3},{8,12},{9,13},{10,... | collective-permute-start | bytes 24584 | tf_op jit(solution)/shard_map/ppermute | solution.py:64
  61.1 5.1 %collective-permute-done.6 = f32[2048]{0:T(1024)S(1)} collective-permute-done((f32[2048]{0:T(1024)S(1)}, f32[2048]{0:T(1024)S(1)}, u32[]{:S(2)}, u32[]{:S(2)}) %collective-permute-start.6) | collective-permute-done | bytes 8224 | tf_op jit(solution)/shard_map/ppermute | solution.py:64
  66.1 1.3 %collective-permute-start.7 = (f32[2048]{0:T(1024)S(1)}, f32[2048]{0:T(1024)S(1)}, u32[]{:S(2)}, u32[]{:S(2)}) collective-permute-start(f32[2048]{0:T(1024)S(1)} %select_add_fusion.3), channel_id=1, source_target_pairs={{0,4},{1,5},{2,6},{3,7},{4,0},{5,1},{6,2},{7,3},{8,12},{9,13},{10,... | collective-permute-start | bytes 24584 | tf_op jit(solution)/shard_map/ppermute | solution.py:69
  67.5 5.1 %collective-permute-done.7 = f32[2048]{0:T(1024)S(1)} collective-permute-done((f32[2048]{0:T(1024)S(1)}, f32[2048]{0:T(1024)S(1)}, u32[]{:S(2)}, u32[]{:S(2)}) %collective-permute-start.7) | collective-permute-done | bytes 8224 | tf_op jit(solution)/shard_map/ppermute | solution.py:69
  72.6 3.5 %collective-permute-done.8 = f32[4096]{0:T(1024)S(1)} collective-permute-done((f32[4096]{0:T(1024)S(1)}, f32[4096]{0:T(1024)S(1)}, u32[]{:S(2)}, u32[]{:S(2)}) %collective-permute-start.8) | collective-permute-done | bytes 16416 | tf_op jit(solution)/shard_map/ppermute | solution.py:69
  76.1 2.8 %collective-permute-done.9 = f32[8192]{0:T(1024)S(1)} collective-permute-done((f32[8192]{0:T(1024)S(1)}, f32[8192]{0:T(1024)S(1)}, u32[]{:S(2)}, u32[]{:S(2)}) %collective-permute-start.9) | collective-permute-done | bytes 32800 | tf_op jit(solution)/shard_map/ppermute | solution.py:69
  78.8 1.4 %collective-permute-start.10 = (f32[16384]{0:T(1024)S(1)}, f32[16384]{0:T(1024)S(1)}, u32[]{:S(2)}, u32[]{:S(2)}) collective-permute-start(f32[16384]{0:T(1024)S(1)} %maximum_select_fusion.3), channel_id=1, source_target_pairs={{0,16},{8,24},{16,0},{24,8},{1,17},{9,25},{17,1},{25,9},{2,18},{10... | collective-permute-start | bytes 196616 | tf_op jit(solution)/shard_map/ppermute | solution.py:69
  80.3 3.2 %collective-permute-done.10 = f32[16384]{0:T(1024)S(1)} collective-permute-done((f32[16384]{0:T(1024)S(1)}, f32[16384]{0:T(1024)S(1)}, u32[]{:S(2)}, u32[]{:S(2)}) %collective-permute-start.10) | collective-permute-done | bytes 65568 | tf_op jit(solution)/shard_map/ppermute | solution.py:69
  83.5 9.6 %collective-permute-start.11 = (f32[32768]{0:T(1024)S(1)}, f32[32768]{0:T(1024)S(1)}, u32[]{:S(2)}, u32[]{:S(2)}) collective-permute-start(f32[32768]{0:T(1024)S(1)} %maximum_select_fusion.1), channel_id=1, source_target_pairs={{0,8},{8,0},{16,24},{24,16},{1,9},{9,1},{17,25},{25,17},{2,10},{10... | collective-permute-start | bytes 393224 | tf_op jit(solution)/shard_map/ppermute | solution.py:69
  (48 shorter events, 13.7 us)
Async XLA Ops:
  1.8 12.6 %copy-start = (bf16[2,3,8,8,32,128]{5,4,3,2,1,0:T(8,128)(2,1)S(1)}, bf16[2,3,8,8,32,128]{5,4,3,2,1,0:T(8,128)(2,1)}, u32[]{:S(2)}) copy-start(bf16[2,3,8,8,32,128]{5,4,3,2,1,0:T(8,128)(2,1)} %param.3) | copy-start | bytes 9437188
  1.8 17.1 %collective-permute-start = (bf16[2,3,1,8,32,128]{5,4,3,2,1,0:T(8,128)(2,1)}, bf16[2,3,1,8,32,128]{5,4,3,2,1,0:T(8,128)(2,1)}, u32[]{:S(2)}, u32[]{:S(2)}) collective-permute-start(bf16[2,3,1,8,32,128]{5,4,3,2,1,0:T(8,128)(2,1)} %slice.218), channel_id=1, source_target_pairs={{0,24},{8,0},{16,8},{24,16},{1,25},{9,1},{17,9},{25,17},{2,26},{10... | collective-permute-start | bytes 1179656 | tf_op jit(solution)/shard_map/ppermute | solution.py:12
  6.1 25.6 %collective-permute-start.1 = (bf16[2,3,8,1,32,128]{5,4,3,2,1,0:T(8,128)(2,1)S(1)}, bf16[2,3,8,1,32,128]{5,4,3,2,1,0:T(8,128)(2,1)}, u32[]{:S(2)}, u32[]{:S(2)}) collective-permute-start(bf16[2,3,8,1,32,128]{5,4,3,2,1,0:T(8,128)(2,1)S(1)} %slice.244), channel_id=1, source_target_pairs={{0,7},{1,0},{2,1},{3,2},{4,3},{5,4},{6,5},{7,6},{8,15},{9,8},{10,9... | collective-permute-start | bytes 1179656 | tf_op jit(solution)/shard_map/ppermute | solution.py:12
  30.6 1.8 %copy-start.1 = (bf16[2,3,8,7,32,128]{5,4,3,2,1,0:T(8,128)(2,1)S(1)}, bf16[2,3,8,7,32,128]{5,4,3,2,1,0:T(8,128)(2,1)}, u32[]{:S(2)}) copy-start(bf16[2,3,8,7,32,128]{5,4,3,2,1,0:T(8,128)(2,1)} %slice.243) | copy-start | bytes 8257540
  44.7 3.7 %collective-permute-start.2 = (f32[32768]{0:T(1024)S(1)}, f32[32768]{0:T(1024)S(1)}, u32[]{:S(2)}, u32[]{:S(2)}) collective-permute-start(f32[32768]{0:T(1024)S(1)} %bitcast.166), channel_id=1, source_target_pairs={{0,8},{8,0},{16,24},{24,16},{1,9},{9,1},{17,25},{25,17},{2,10},{10... | collective-permute-start | bytes 393224 | tf_op jit(solution)/shard_map/ppermute | solution.py:64
  48.4 4.7 %collective-permute-start.3 = (f32[16384]{0:T(1024)S(1)}, f32[16384]{0:T(1024)S(1)}, u32[]{:S(2)}, u32[]{:S(2)}) collective-permute-start(f32[16384]{0:T(1024)S(1)} %slice_select_fusion.2), channel_id=1, source_target_pairs={{0,16},{8,24},{16,0},{24,8},{1,17},{9,25},{17,1},{25,9},{2,18},{10... | collective-permute-start | bytes 196616 | tf_op jit(solution)/shard_map/ppermute | solution.py:64
  53.2 2.9 %collective-permute-start.4 = (f32[8192]{0:T(1024)S(1)}, f32[8192]{0:T(1024)S(1)}, u32[]{:S(2)}, u32[]{:S(2)}) collective-permute-start(f32[8192]{0:T(1024)S(1)} %slice_select_fusion.3), channel_id=1, source_target_pairs={{0,1},{1,0},{2,3},{3,2},{4,5},{5,4},{6,7},{7,6},{8,9},{9,8},{10,11... | collective-permute-start | bytes 98312 | tf_op jit(solution)/shard_map/ppermute | solution.py:64
  56.0 3.6 %collective-permute-start.5 = (f32[4096]{0:T(1024)S(1)}, f32[4096]{0:T(1024)S(1)}, u32[]{:S(2)}, u32[]{:S(2)}) collective-permute-start(f32[4096]{0:T(1024)S(1)} %slice_select_fusion.4), channel_id=1, source_target_pairs={{0,2},{1,3},{2,0},{3,1},{4,6},{5,7},{6,4},{7,5},{8,10},{9,11},{10,... | collective-permute-start | bytes 49160 | tf_op jit(solution)/shard_map/ppermute | solution.py:64
  59.6 6.5 %collective-permute-start.6 = (f32[2048]{0:T(1024)S(1)}, f32[2048]{0:T(1024)S(1)}, u32[]{:S(2)}, u32[]{:S(2)}) collective-permute-start(f32[2048]{0:T(1024)S(1)} %slice_select_fusion.5), channel_id=1, source_target_pairs={{0,4},{1,5},{2,6},{3,7},{4,0},{5,1},{6,2},{7,3},{8,12},{9,13},{10,... | collective-permute-start | bytes 24584 | tf_op jit(solution)/shard_map/ppermute | solution.py:64
  66.1 6.4 %collective-permute-start.7 = (f32[2048]{0:T(1024)S(1)}, f32[2048]{0:T(1024)S(1)}, u32[]{:S(2)}, u32[]{:S(2)}) collective-permute-start(f32[2048]{0:T(1024)S(1)} %select_add_fusion.3), channel_id=1, source_target_pairs={{0,4},{1,5},{2,6},{3,7},{4,0},{5,1},{6,2},{7,3},{8,12},{9,13},{10,... | collective-permute-start | bytes 24584 | tf_op jit(solution)/shard_map/ppermute | solution.py:69
  72.5 3.5 %collective-permute-start.8 = (f32[4096]{0:T(1024)S(1)}, f32[4096]{0:T(1024)S(1)}, u32[]{:S(2)}, u32[]{:S(2)}) collective-permute-start(f32[4096]{0:T(1024)S(1)} %maximum_select_fusion.7), channel_id=1, source_target_pairs={{0,2},{1,3},{2,0},{3,1},{4,6},{5,7},{6,4},{7,5},{8,10},{9,11},{10,... | collective-permute-start | bytes 49160 | tf_op jit(solution)/shard_map/ppermute | solution.py:69
  76.0 2.8 %collective-permute-start.9 = (f32[8192]{0:T(1024)S(1)}, f32[8192]{0:T(1024)S(1)}, u32[]{:S(2)}, u32[]{:S(2)}) collective-permute-start(f32[8192]{0:T(1024)S(1)} %maximum_select_fusion.5), channel_id=1, source_target_pairs={{0,1},{1,0},{2,3},{3,2},{4,5},{5,4},{6,7},{7,6},{8,9},{9,8},{10,11... | collective-permute-start | bytes 98312 | tf_op jit(solution)/shard_map/ppermute | solution.py:69
  78.8 4.7 %collective-permute-start.10 = (f32[16384]{0:T(1024)S(1)}, f32[16384]{0:T(1024)S(1)}, u32[]{:S(2)}, u32[]{:S(2)}) collective-permute-start(f32[16384]{0:T(1024)S(1)} %maximum_select_fusion.3), channel_id=1, source_target_pairs={{0,16},{8,24},{16,0},{24,8},{1,17},{9,25},{17,1},{25,9},{2,18},{10... | collective-permute-start | bytes 196616 | tf_op jit(solution)/shard_map/ppermute | solution.py:69
  83.5 10.6 %collective-permute-start.11 = (f32[32768]{0:T(1024)S(1)}, f32[32768]{0:T(1024)S(1)}, u32[]{:S(2)}, u32[]{:S(2)}) collective-permute-start(f32[32768]{0:T(1024)S(1)} %maximum_select_fusion.1), channel_id=1, source_target_pairs={{0,8},{8,0},{16,24},{24,16},{1,9},{9,1},{17,25},{25,17},{2,10},{10... | collective-permute-start | bytes 393224 | tf_op jit(solution)/shard_map/ppermute | solution.py:69

commit v2 on v0

--- a/solution.py
+++ b/solution.py
@@ -47,6 +47,16 @@
     )
 
 
+def reduce_partials(x):
+    shape = x.shape
+    n = lax.axis_size("gx") * lax.axis_size("yz")
+    chunks = x.reshape(n, -1)
+    got = lax.all_to_all(chunks, ("gx", "yz"), 0, 0, tiled=True)
+    total = jnp.sum(got, 0, keepdims=True)
+    every = jnp.broadcast_to(total, (n, total.shape[1]))
+    return lax.all_to_all(every, ("gx", "yz"), 0, 0, tiled=True).reshape(shape)
+
+
 def local(vectors, gauge_x, gauge_y):
     nvecs = vectors.shape[-1]
     from_next_x = shifted(vectors[:, :, :1], "gx", -1)
@@ -57,9 +67,7 @@
     image_y = colour_apply(gauge_y, shifted_y)
     left_rows = vectors.reshape(-1, nvecs)
     blocks = right_block(image_x) + right_block(image_y)
-    summed = lax.psum(
-        jnp.concatenate([contract(left_rows, member) for member in blocks], 1), ("gx", "yz")
-    )
+    summed = reduce_partials(jnp.concatenate([contract(left_rows, member) for member in blocks], 1))
     sites_total = (
         vectors.shape[2]
         * lax.axis_size("gx")

time: 315 us -> 74.6 us (0.24)
  waiting for transfers between devices: 263 us -> 0.01 us
  blocking collectives: 0 us -> 39.6 us
  between operations: 13.6 us -> 0.2 us
    psum x1 -> x0, waiting for transfers between devices: 263 us -> none  [local(): lax.psum(jnp.concatenate([contract(left_rows, member) for member in block...]
    all_to_all x0 -> x2, blocking collectives: none -> 39.6 us  [the longest x1 22.7 us: reduce_partials(): got = lax.all_to_all(chunks, ('gx', 'yz'), 0, 0, tiled=True)]
  transfers between devices with their start and end apart: 3 -> 2, of which waited for: 1 -> 0; matrix products, arithmetic and copies ran while one was open for 4% -> 17% of each run, Pallas kernels for 0% -> 0%
where the time goes in v2:
time: 74.6 us; the launch traced here: 74.3 us
  blocking collectives  39.6 us (53%)
  other arithmetic  17.5 us (23%)
  starting transfers between devices  7.42 us (10%)
  local copies, waits for them, and re-layouts  5.46 us (7%)
  matrix products  4.18 us (6%)
    all_to_all x1, blocking collectives, reduce_partials(): got = lax.all_to_all(chunks, ('gx', 'yz'), 0, 0, tiled=True)  22.7 us
    all_to_all x1, blocking collectives, reduce_partials(): return lax.all_to_all(every, ('gx', 'yz'), 0, 0, tiled=True).reshape(shape)  16.9 us
    another operation x6, other arithmetic  15.8 us
    ppermute x2, starting transfers between devices, shifted(): return lax.ppermute(value, axis, pairs)  7.42 us
    dot_general x4, matrix products, contract(): lax.dot_general(left_cols, right_cols, (((0,), (0,)), ((), ())), preferre...  4.18 us
  transfers between devices with their start and end apart: 2, of which 0 were waited for; matrix products, arithmetic and copies ran while one was open for 17% of the time, Pallas kernels for 0%

profile of v2, /device:TPU:1, one launch (start us, length us, event | category | flops | bytes accessed | tf_op | source)
XLA Modules:
  0.0 74.3 jit_solution(11503123691710930986)
XLA Ops:
  0.0 1.0 %slice.186 = bf16[2,3,1,8,32,128]{5,4,3,2,1,0:T(8,128)(2,1)S(1)} slice(bf16[2,3,8,8,32,128]{5,4,3,2,1,0:T(8,128)(2,1)} %param.3), slice={[0:2], [0:3], [0:1], [0:8], [0:32], [0:128]} | slice | bytes 786432 | tf_op jit(solution)/shard_map/slice | solution.py:62
  1.0 3.3 %collective-permute-start = (bf16[2,3,1,8,32,128]{5,4,3,2,1,0:T(8,128)(2,1)S(1)}, bf16[2,3,1,8,32,128]{5,4,3,2,1,0:T(8,128)(2,1)S(1)}, u32[]{:S(2)}, u32[]{:S(2)}) collective-permute-start(bf16[2,3,1,8,32,128]{5,4,3,2,1,0:T(8,128)(2,1)S(1)} %slice.186), channel_id=1, source_target_pairs={{0,24},{8,0},{16,8},{24,16},{1,25},{9,1},{17,9},{25,17},{2,26},{10... | collective-permute-start | bytes 1179656 | tf_op jit(solution)/shard_map/ppermute | solution.py:12
  4.4 1.0 %slice.212 = bf16[2,3,8,1,32,128]{5,4,3,2,1,0:T(8,128)(2,1)S(1)} slice(bf16[2,3,8,8,32,128]{5,4,3,2,1,0:T(8,128)(2,1)} %param.3), slice={[0:2], [0:3], [0:8], [0:1], [0:32], [0:128]} | slice | bytes 786432 | tf_op jit(solution)/shard_map/slice | solution.py:64
  5.4 4.1 %collective-permute-start.1 = (bf16[2,3,8,1,32,128]{5,4,3,2,1,0:T(8,128)(2,1)S(1)}, bf16[2,3,8,1,32,128]{5,4,3,2,1,0:T(8,128)(2,1)S(1)}, u32[]{:S(2)}, u32[]{:S(2)}) collective-permute-start(bf16[2,3,8,1,32,128]{5,4,3,2,1,0:T(8,128)(2,1)S(1)} %slice.212), channel_id=1, source_target_pairs={{0,7},{1,0},{2,1},{3,2},{4,3},{5,4},{6,5},{7,6},{8,15},{9,8},{10,9... | collective-permute-start | bytes 1179656 | tf_op jit(solution)/shard_map/ppermute | solution.py:12
  9.5 0.7 slice.211
  10.2 0.4 copy-done.1
  10.8 0.8 %slice-done = bf16[2,3,7,8,32,128]{5,4,3,2,1,0:T(8,128)(2,1)S(1)} async-done(((bf16[2,3,8,8,32,128]{5,4,3,2,1,0:T(8,128)(2,1)}), bf16[2,3,7,8,32,128]{5,4,3,2,1,0:T(8,128)(2,1)S(1)}, s32[]{:S(2)}) %slice-start) | async-done | bytes 2752536 | tf_op jit(solution)/shard_map/slice | solution.py:63
  11.6 2.1 %fusion.51 = (bf16[1,8,8,32,128]{4,3,2,1,0:T(8,128)(2,1)S(1)}, bf16[1,8,8,32,128]{4,3,2,1,0:T(8,128)(2,1)S(1)}, bf16[1,8,8,32,128]{4,3,2,1,0:T(8,128)(2,1)S(1)},...) fusion(f32[8,8,32]{2,1,0:T(8,128)S(1)} %get-tuple-element.41, ...), kind=kLoop, calls=%fused_computation.139 | loop fusion | flops 6291456 | bytes 6864896 | tf_op jit(solution)/shard_map/convert.25
  13.7 1.9 %fusion.33 = bf16[1,8,8,32,128]{4,3,2,1,0:T(8,128)(2,1)S(1)} fusion(bf16[1,8,8,32,128]{4,3,2,1,0:T(8,128)(2,1)S(1)} %get-tuple-element.11, bf16[1,8,8,32,128]{4,3,2,1,0:T(8,128)(2,1)S(1)} %get-tuple-element.10, bf16[1,8,8,32,128]{4,3,2,1,0:T(8,128)(2,1)S(1)} %get-tuple-element.9, bf16[1,8,8,32,128]{4,3,2,1,0:T(8,128)(2,1)S(1)} %get-tuple-element.8, ...), kind=kLoop, calls=%fused_computation.121 | loop fusion | flops 4718592 | bytes 3719168 | tf_op jit(solution)/shard_map/convert.29
  15.7 3.9 %fusion.57 = (bf16[1,8,8,32,128]{4,3,2,1,0:T(8,128)(2,1)S(1)}, bf16[1,8,8,32,128]{4,3,2,1,0:T(8,128)(2,1)S(1)}, bf16[1,8,8,32,128]{4,3,2,1,0:T(8,128)(2,1)S(1)}, bf16[1,8,8,32,128]{4,3,2,1,0:T(8,128)(2,1)S(1)}) fusion(bf16[1,8,8,32,128]{4,3,2,1,0:T(8,128)(2,1)S(1)} %get-tuple-element.11, bf16[1,8,8,32,128]{4,3,2,1,0:T(8,128)(2,1)S(1)} %get-tuple-element.10, ...), kind=kLoop, calls=%fused_computation.145 | loop fusion | flops 14155776 | bytes 5341184 | tf_op jit(solution)/shard_map/convert.26
  19.6 0.3 pad_maximum_fusion
  19.9 0.3 bitcast_negate_fusion.1
  20.2 1.0 %fusion.25 = f32[128,128]{0,1:T(8,128)S(1)} fusion(bf16[12288,128]{1,0:T(8,128)(2,1)S(1)} %bitcast.142, bf16[6144,128]{1,0:T(8,128)(2,1)S(1)} %bitcast.148, bf16[6144,128]{1,0:T(8,128)(2,1)S(1)} %bitcast.146), kind=kOutput, calls=%fused_computation.115 | convolution fusion | flops 408944640 | bytes 6356992 | tf_op jit(solution)/shard_map/dot_general | solution.py:45
  21.3 1.0 %fusion.22 = f32[128,128]{0,1:T(8,128)S(1)} fusion(bf16[12288,128]{1,0:T(8,128)(2,1)S(1)} %bitcast.143, bf16[6144,128]{1,0:T(8,128)(2,1)S(1)} %bitcast_negate_fusion.1, bf16[6144,128]{1,0:T(8,128)(2,1)S(1)} %bitcast.149), kind=kOutput, calls=%fused_computation.114 | convolution fusion | flops 408944640 | bytes 6356992 | tf_op jit(solution)/shard_map/dot_general | solution.py:45
  22.3 2.0 %fusion.87 = (bf16[1,8,8,32,128]{4,3,2,1,0:T(8,128)(2,1)S(1)}, bf16[1,8,8,32,128]{4,3,2,1,0:T(8,128)(2,1)S(1)}, bf16[1,8,8,32,128]{4,3,2,1,0:T(8,128)(2,1)S(1)},...) fusion(f32[8,8,32]{2,1,0:T(8,128)S(1)} %get-tuple-element.59, ...), kind=kLoop, calls=%fused_computation.175 | loop fusion | flops 6291456 | bytes 6864896 | tf_op jit(solution)/shard_map/convert.15
  24.4 1.9 %fusion.69 = bf16[1,8,8,32,128]{4,3,2,1,0:T(8,128)(2,1)S(1)} fusion(bf16[1,8,8,32,128]{4,3,2,1,0:T(8,128)(2,1)S(1)} %get-tuple-element.18, bf16[1,8,8,32,128]{4,3,2,1,0:T(8,128)(2,1)S(1)} %get-tuple-element.17, bf16[1,8,8,32,128]{4,3,2,1,0:T(8,128)(2,1)S(1)} %get-tuple-element.16, bf16[1,8,8,32,128]{4,3,2,1,0:T(8,128)(2,1)S(1)} %get-tuple-element.15, ...), kind=kLoop, calls=%fused_computation.157 | loop fusion | flops 4718592 | bytes 3719168 | tf_op jit(solution)/shard_map/convert.19
  26.3 3.9 %fusion.93 = (bf16[1,8,8,32,128]{4,3,2,1,0:T(8,128)(2,1)S(1)}, bf16[1,8,8,32,128]{4,3,2,1,0:T(8,128)(2,1)S(1)}, bf16[1,8,8,32,128]{4,3,2,1,0:T(8,128)(2,1)S(1)}, bf16[1,8,8,32,128]{4,3,2,1,0:T(8,128)(2,1)S(1)}) fusion(bf16[1,8,8,32,128]{4,3,2,1,0:T(8,128)(2,1)S(1)} %get-tuple-element.18, bf16[1,8,8,32,128]{4,3,2,1,0:T(8,128)(2,1)S(1)} %get-tuple-element.17, ...), kind=kLoop, calls=%fused_computation.181 | loop fusion | flops 14155776 | bytes 5341184 | tf_op jit(solution)/shard_map/convert.16
  30.2 0.3 pad_maximum_fusion.2
  30.6 0.3 bitcast_negate_fusion
  30.9 1.0 %fusion.19 = f32[128,128]{0,1:T(8,128)S(1)} fusion(bf16[12288,128]{1,0:T(8,128)(2,1)S(1)} %bitcast.144, bf16[6144,128]{1,0:T(8,128)(2,1)S(1)} %bitcast.150, bf16[6144,128]{1,0:T(8,128)(2,1)S(1)} %bitcast.147), kind=kOutput, calls=%fused_computation.113 | convolution fusion | flops 408944640 | bytes 6356992 | tf_op jit(solution)/shard_map/dot_general | solution.py:45
  31.9 1.1 %fusion.16 = f32[128,128]{0,1:T(8,128)S(1)} fusion(bf16[12288,128]{1,0:T(8,128)(2,1)S(1)} %bitcast.145, bf16[6144,128]{1,0:T(8,128)(2,1)S(1)} %bitcast_negate_fusion, bf16[6144,128]{1,0:T(8,128)(2,1)S(1)} %bitcast.151), kind=kOutput, calls=%fused_computation.112 | convolution fusion | flops 408944640 | bytes 6356992 | tf_op jit(solution)/shard_map/dot_general | solution.py:45
  33.5 22.7 %all_to_all.16 = f32[32,1,2048]{2,1,0:T(1,128)S(1)} all-to-all(f32[32,1,2048]{2,1,0:T(1,128)S(1)} %all_to_all.13), channel_id=1, replica_groups=mesh['ta'=8,'gx'=4,'yz'=8] {'gx','yz'}, dimensions={0} | all-to-all | bytes 524288 | tf_op jit(solution)/shard_map/all_to_all | solution.py:54
  56.5 16.9 %all_to_all.17 = f32[32,1,2048]{2,1,0:T(1,128)S(1)} all-to-all(f32[32,1,2048]{2,1,0:T(1,128)S(1)} %broadcast_in_dim.2), channel_id=1, replica_groups=mesh['ta'=8,'gx'=4,'yz'=8] {'gx','yz'}, dimensions={0} | all-to-all | bytes 524288 | tf_op jit(solution)/shard_map/all_to_all | solution.py:57
  73.6 0.7 copy.8
  (16 shorter events, 1.3 us)
Async XLA Ops:
  1.0 8.5 %copy-start = (bf16[2,3,8,8,32,128]{5,4,3,2,1,0:T(8,128)(2,1)S(1)}, bf16[2,3,8,8,32,128]{5,4,3,2,1,0:T(8,128)(2,1)}, u32[]{:S(2)}) copy-start(bf16[2,3,8,8,32,128]{5,4,3,2,1,0:T(8,128)(2,1)} %param.3) | copy-start | bytes 9437188
  1.0 9.8 %collective-permute-start = (bf16[2,3,1,8,32,128]{5,4,3,2,1,0:T(8,128)(2,1)S(1)}, bf16[2,3,1,8,32,128]{5,4,3,2,1,0:T(8,128)(2,1)S(1)}, u32[]{:S(2)}, u32[]{:S(2)}) collective-permute-start(bf16[2,3,1,8,32,128]{5,4,3,2,1,0:T(8,128)(2,1)S(1)} %slice.186), channel_id=1, source_target_pairs={{0,24},{8,0},{16,8},{24,16},{1,25},{9,1},{17,9},{25,17},{2,26},{10... | collective-permute-start | bytes 1179656 | tf_op jit(solution)/shard_map/ppermute | solution.py:12
  5.4 16.9 %collective-permute-start.1 = (bf16[2,3,8,1,32,128]{5,4,3,2,1,0:T(8,128)(2,1)S(1)}, bf16[2,3,8,1,32,128]{5,4,3,2,1,0:T(8,128)(2,1)S(1)}, u32[]{:S(2)}, u32[]{:S(2)}) collective-permute-start(bf16[2,3,8,1,32,128]{5,4,3,2,1,0:T(8,128)(2,1)S(1)} %slice.212), channel_id=1, source_target_pairs={{0,7},{1,0},{2,1},{3,2},{4,3},{5,4},{6,5},{7,6},{8,15},{9,8},{10,9... | collective-permute-start | bytes 1179656 | tf_op jit(solution)/shard_map/ppermute | solution.py:12
  9.5 1.1 %copy-start.1 = (f32[2,3,3,8,8,32]{5,4,3,2,1,0:T(8,128)S(1)}, f32[2,3,3,8,8,32]{5,4,3,2,1,0:T(8,128)}, u32[]{:S(2)}) copy-start(f32[2,3,3,8,8,32]{5,4,3,2,1,0:T(8,128)} %param.4) | copy-start | bytes 442372
  9.5 1.2 %copy-start.2 = (f32[2,3,3,8,8,32]{5,4,3,2,1,0:T(8,128)S(1)}, f32[2,3,3,8,8,32]{5,4,3,2,1,0:T(8,128)}, u32[]{:S(2)}) copy-start(f32[2,3,3,8,8,32]{5,4,3,2,1,0:T(8,128)} %param.5) | copy-start | bytes 442372
  9.5 2.1 %slice-start = ((bf16[2,3,8,8,32,128]{5,4,3,2,1,0:T(8,128)(2,1)}), bf16[2,3,7,8,32,128]{5,4,3,2,1,0:T(8,128)(2,1)S(1)}, s32[]{:S(2)}) async-start(bf16[2,3,8,8,32,128]{5,4,3,2,1,0:T(8,128)(2,1)} %param.3), calls=%async_computation.2 | async-start | bytes 5505024 | tf_op jit(solution)/shard_map/slice | solution.py:63

commit v3 on v2

v3 whole, which is shorter than its diff:
```python
import math

import jax
import jax.numpy as jnp
from jax import lax
from jax.experimental import pallas as pl
from jax.experimental.pallas import tpu as pltpu
from jax.sharding import PartitionSpec as P


def shifted(value, axis, steps):
    count = lax.axis_size(axis)
    pairs = [(source, (source + steps) % count) for source in range(count)]
    return lax.ppermute(value, axis, pairs)


def elementals_kernel(scaling, v_ref, hx_ref, hy_ref, g_ref, o_ref, vt_ref, wy_ref, r_ref, acc_a, acc_b):
    planes, lines, row, vecs = v_ref.shape[2:]
    sites = lines * row
    step = 16
    nt = (((1,), (1,)), ((), ()))

    def transpose_plane(p, carry):
        for c in range(2):
            for a in range(3):
                vt_ref[c, a, p] = v_ref[c, a, p].reshape(sites, vecs).T
                inner = v_ref[c, a, p, 1:].reshape(sites - row, vecs)
                wy_ref[c, a, p] = jnp.concatenate([inner, hy_ref[c, a, p, 0]], 0).T
        return carry

    lax.fori_loop(0, planes, transpose_plane, 0)
    for c in range(2):
        for a in range(3):
            vt_ref[c, a, planes] = hx_ref[c, a, 0].reshape(sites, vecs).T
    acc_a[...] = jnp.zeros_like(acc_a)
    acc_b[...] = jnp.zeros_like(acc_b)

    def plane(p, carry):
        def rows_block(jc, inner_carry):
            j0 = pl.multiple_of(jc * step, step)
            sources = (
                lambda c, b: vt_ref[c, b, p + 1, pl.ds(j0, step), :],
                lambda c, b: wy_ref[c, b, p, pl.ds(j0, step), :],
            )
            for d in range(2):
                w_re = [sources[d](0, b).astype(jnp.float32) for b in range(3)]
                w_im = [sources[d](1, b).astype(jnp.float32) for b in range(3)]
                for a in range(3):
                    re = None
                    im = None
                    for b in range(3):
                        k = d * 18 + a * 3 + b
                        gr = g_ref[p, k : k + 1, :]
                        gi = g_ref[p, k + 9 : k + 10, :]
                        t_re = gr * w_re[b] - gi * w_im[b]
                        t_im = gr * w_im[b] + gi * w_re[b]
                        re = t_re if re is None else re + t_re
                        im = t_im if im is None else im + t_im
                    r_ref[a, pl.ds(2 * d * vecs + j0, step), :] = re.astype(jnp.bfloat16)
                    r_ref[a, pl.ds((2 * d + 1) * vecs + j0, step), :] = im.astype(jnp.bfloat16)
            return inner_carry

        lax.fori_loop(0, vecs // step, rows_block, 0)
        for a in range(3):
            right = r_ref[a]
            acc_a[...] += lax.dot_general(vt_ref[0, a, p], right, nt, preferred_element_type=jnp.float32)
            acc_b[...] += lax.dot_general(vt_ref[1, a, p], right, nt, preferred_element_type=jnp.float32)
        return carry

    lax.fori_loop(0, planes, plane, 0)
    a = acc_a[...]
    b = acc_b[...]
    for d in range(2):
        o = 2 * d * vecs
        o_ref[d, 0] = (a[:, o : o + vecs] + b[:, o + vecs : o + 2 * vecs]) * scaling
        o_ref[d, 1] = (a[:, o + vecs : o + 2 * vecs] - b[:, o : o + vecs]) * scaling


def site_rows(gauge_x, gauge_y):
    nx, ny, nz = gauge_x.shape[3:]
    both = jnp.concatenate([gauge_x.reshape(18, nx, ny * nz), gauge_y.reshape(18, nx, ny * nz)], 0)
    return jnp.transpose(both, (1, 0, 2))


def partials(vectors, from_next_x, from_next_y, gauge_x, gauge_y, scaling):
    nx, ny, nz, nv = vectors.shape[2:]
    sites = ny * nz
    vmem = pltpu.MemorySpace.VMEM
    return pl.pallas_call(
        lambda *refs: elementals_kernel(scaling, *refs),
        out_shape=jax.ShapeDtypeStruct((2, 2, nv, nv), jnp.float32),
        in_specs=[pl.BlockSpec(memory_space=vmem)] * 4,
        out_specs=pl.BlockSpec(memory_space=vmem),
        scratch_shapes=[
            pltpu.VMEM((2, 3, nx + 1, nv, sites), jnp.bfloat16),
            pltpu.VMEM((2, 3, nx, nv, sites), jnp.bfloat16),
            pltpu.VMEM((3, 4 * nv, sites), jnp.bfloat16),
            pltpu.VMEM((nv, 4 * nv), jnp.float32),
            pltpu.VMEM((nv, 4 * nv), jnp.float32),
        ],
    )(vectors, from_next_x, from_next_y, site_rows(gauge_x, gauge_y))


def reduce_partials(x):
    shape = x.shape
    n = lax.axis_size("gx") * lax.axis_size("yz")
    chunks = x.reshape(n, -1, shape[-1])
    got = lax.all_to_all(chunks, ("gx", "yz"), 0, 0, tiled=True)
    total = jnp.sum(got, 0, keepdims=True)
    every = jnp.broadcast_to(total, chunks.shape)
    return lax.all_to_all(every, ("gx", "yz"), 0, 0, tiled=True).reshape(shape)


def local(vectors, gauge_x, gauge_y):
    from_next_x = shifted(vectors[:, :, :1], "gx", -1)
    from_next_y = shifted(vectors[:, :, :, :1], "yz", -1)
    sites_total = (
        vectors.shape[2]
        * lax.axis_size("gx")
        * vectors.shape[3]
        * lax.axis_size("yz")
        * vectors.shape[4]
    )
    scaling = 1.0 / math.sqrt(3.0 * sites_total)
    return reduce_partials(partials(vectors, from_next_x, from_next_y, gauge_x, gauge_y, scaling))


def solution(mesh):
    placed = (
        P(None, None, "gx", "yz", "ta", None),
        P(None, None, None, "gx", "yz", "ta"),
        P(None, None, None, "gx", "yz", "ta"),
    )
    return jax.shard_map(
        local, mesh=mesh, in_specs=placed, out_specs=P("ta", None, None, None), check_vma=False
    )
```

time: 74.6 us -> 73.6 us (0.987)
  other arithmetic: 17.5 us -> 0.79 us
  Pallas kernels: 0 us -> 15.8 us
  matrix products: 4.18 us -> 0 us
  waiting for transfers between devices: 0.01 us -> 2.68 us
  blocking collectives: 39.6 us -> 40.5 us
    another operation x8 -> x0, other arithmetic: 16.5 us -> none
    pallas_call x0 -> x1, Pallas kernels: none -> 15.8 us  [partials(): pl.pallas_call(lambda *refs: elementals_kernel(scaling, *refs), out_shape...]
    dot_general x4 -> x0, matrix products: 4.18 us -> none  [contract(): lax.dot_general(left_cols, right_cols, (((0,), (0,)), ((), ())), preferre...]
    ppermute x2, waiting for transfers between devices: 0.01 us -> 2.68 us  [shifted(): return lax.ppermute(value, axis, pairs)]
    reshape x0 -> x4, local copies, waits for them, and re-layouts: none -> 2.62 us  [the longest x2 1.31 us: site_rows(): gauge_x.reshape(18, nx, ny * nz)]
    slice x3 -> x0, local copies, waits for them, and re-layouts: 1.54 us -> none  [the longest x2 0.84 us: local(): shifted_x = jnp.concatenate([vectors[:, :, 1:], from_next_x], 2)]
    unnamed x6 -> x5, local copies, waits for them, and re-layouts: 0.49 us -> 1.44 us
    all_to_all x1, blocking collectives: 22.7 us -> 23.6 us  [reduce_partials(): got = lax.all_to_all(chunks, ('gx', 'yz'), 0, 0, tiled=True)]
  transfers between devices with their start and end apart: 2 -> 2, of which waited for: 0 -> 1; matrix products, arithmetic and copies ran while one was open for 17% -> 6% of each run, Pallas kernels for 0% -> 0%
where the time goes in v3:
time: 73.6 us; the launch traced here: 73.2 us
  blocking collectives  40.5 us (55%)
  Pallas kernels  15.8 us (21%)
  starting transfers between devices  7.23 us (10%)
  local copies, waits for them, and re-layouts  6.13 us (8%)
  waiting for transfers between devices  2.68 us (4%)
  other arithmetic  0.79 us (1%)
    all_to_all x1, blocking collectives, reduce_partials(): got = lax.all_to_all(chunks, ('gx', 'yz'), 0, 0, tiled=True)  23.6 us
    all_to_all x1, blocking collectives, reduce_partials(): return lax.all_to_all(every, ('gx', 'yz'), 0, 0, tiled=True).reshape(shape)  16.9 us
    pallas_call x1, Pallas kernels, partials(): pl.pallas_call(lambda *refs: elementals_kernel(scaling, *refs), out_shape...  15.8 us
    ppermute x2, starting transfers between devices, shifted(): return lax.ppermute(value, axis, pairs)  7.23 us
    ppermute x2, waiting for transfers between devices, shifted(): return lax.ppermute(value, axis, pairs)  2.68 us
  transfers between devices with their start and end apart: 2, of which 1 were waited for; matrix products, arithmetic and copies ran while one was open for 6% of the time, Pallas kernels for 0%

profile of v3, /device:TPU:1, one launch (start us, length us, event | category | flops | bytes accessed | tf_op | source)
XLA Modules:
  0.0 73.2 jit_solution(8058991203392610465)
XLA Ops:
  0.0 1.0 %slice.6 = bf16[2,3,1,8,32,128]{5,4,3,2,1,0:T(8,128)(2,1)S(1)} slice(bf16[2,3,8,8,32,128]{5,4,3,2,1,0:T(8,128)(2,1)} %refs_0_.1), slice={[0:2], [0:3], [0:1], [0:8], [0:32], [0:128]} | slice | bytes 786432 | tf_op jit(solution)/shard_map/slice | solution.py:115
  1.0 3.3 %collective-permute-start = (bf16[2,3,1,8,32,128]{5,4,3,2,1,0:T(8,128)(2,1)S(1)}, bf16[2,3,1,8,32,128]{5,4,3,2,1,0:T(8,128)(2,1)S(1)}, u32[]{:S(2)}, u32[]{:S(2)}) collective-permute-start(bf16[2,3,1,8,32,128]{5,4,3,2,1,0:T(8,128)(2,1)S(1)} %slice.6), channel_id=1, source_target_pairs={{0,24},{8,0},{16,8},{24,16},{1,25},{9,1},{17,9},{25,17},{2,26},{10... | collective-permute-start | bytes 1179656 | tf_op jit(solution)/shard_map/ppermute | solution.py:14
  4.3 1.0 %slice.7 = bf16[2,3,8,1,32,128]{5,4,3,2,1,0:T(8,128)(2,1)S(1)} slice(bf16[2,3,8,8,32,128]{5,4,3,2,1,0:T(8,128)(2,1)} %refs_0_.1), slice={[0:2], [0:3], [0:8], [0:1], [0:32], [0:128]} | slice | bytes 786432 | tf_op jit(solution)/shard_map/slice | solution.py:116
  5.4 3.9 %collective-permute-start.1 = (bf16[2,3,8,1,32,128]{5,4,3,2,1,0:T(8,128)(2,1)S(1)}, bf16[2,3,8,1,32,128]{5,4,3,2,1,0:T(8,128)(2,1)S(1)}, u32[]{:S(2)}, u32[]{:S(2)}) collective-permute-start(bf16[2,3,8,1,32,128]{5,4,3,2,1,0:T(8,128)(2,1)S(1)} %slice.7), channel_id=1, source_target_pairs={{0,7},{1,0},{2,1},{3,2},{4,3},{5,4},{6,5},{7,6},{8,15},{9,8},{10,9... | collective-permute-start | bytes 1179656 | tf_op jit(solution)/shard_map/ppermute | solution.py:14
  9.3 1.3 %reshape.14 = f32[18,8,256]{2,1,0:T(8,128)S(1)} reshape(f32[2,3,3,8,8,32]{5,4,3,2,1,0:T(8,128)} %param.5) | data formatting | bytes 294912 | tf_op jit(solution)/shard_map/reshape | solution.py:81
  10.6 1.3 %reshape.13 = f32[18,8,256]{2,1,0:T(8,128)S(1)} reshape(f32[2,3,3,8,8,32]{5,4,3,2,1,0:T(8,128)} %param.4) | data formatting | bytes 294912 | tf_op jit(solution)/shard_map/reshape | solution.py:81
  11.9 0.8 %maximum_bitcast_fusion.refs_3_ = f32[8,36,256]{2,1,0:T(8,128)} fusion(f32[18,8,256]{2,0,1:T(8,128)S(1)} %copy.7, f32[18,8,256]{2,0,1:T(8,128)S(1)} %copy.6), kind=kLoop, calls=%fused_computation | loop fusion | flops 73728 | bytes 589824 | tf_op jit(solution)/shard_map/transpose | solution.py:82
  12.7 0.0 collective-permute-done.refs_1_
  12.7 0.0 copy-start
  12.7 2.7 %collective-permute-done.1.refs_2_ = bf16[2,3,8,1,32,128]{5,4,3,2,1,0:T(8,128)(2,1)S(1)} collective-permute-done((bf16[2,3,8,1,32,128]{5,4,3,2,1,0:T(8,128)(2,1)S(1)}, bf16[2,3,8,1,32,128]{5,4,3,2,1,0:T(8,128)(2,1)S(1)}, u32[]{:S(2)}, u32[]{:S(2)}) %collective-permute-start.1) | collective-permute-done | bytes 393248 | tf_op jit(solution)/shard_map/ppermute | solution.py:14
  15.4 0.0 copy-done
  15.4 0.0 copy-start.1
  15.4 0.7 %copy-done.1 = bf16[2,3,8,1,32,128]{5,4,3,2,1,0:T(8,128)(2,1)} copy-done((bf16[2,3,8,1,32,128]{5,4,3,2,1,0:T(8,128)(2,1)}, bf16[2,3,8,1,32,128]{5,4,3,2,1,0:T(8,128)(2,1)S(1)}, u32[]{:S(2)}) %copy-start.1) | copy-done | bytes 393240
  16.1 15.8 %shard_map.37 = f32[2,2,128,128]{3,2,1,0:T(8,128)} custom-call(bf16[2,3,8,8,32,128]{5,4,3,2,1,0:T(8,128)(2,1)} %refs_0_.1, bf16[2,3,1,8,32,128]{5,4,3,2,1,0:T(8,128)(2,1)} %copy-done, bf16[2,3,8,1,32,128]{5,4,3,2,1,0:T(8,128)(2,1)} %copy-done.1, f32[8,36,256]{2,1,0:T(8,128)} %maximum_bitcast_fusion.refs_3_), custom_call_target="tpu_custom_call" | custom-call | tf_op jit(solution)/shard_map/pallas_call | solution.py:89
  32.0 23.6 %all_to_all.10 = f32[32,16,128]{2,1,0:T(8,128)S(1)} all-to-all(f32[32,16,128]{2,1,0:T(8,128)} %bitcast.8), channel_id=1, replica_groups=mesh['ta'=8,'gx'=4,'yz'=8] {'gx','yz'}, dimensions={0} | all-to-all | bytes 524288 | tf_op jit(solution)/shard_map/all_to_all | solution.py:108
  55.6 16.9 %all_to_all.11 = f32[32,16,128]{2,1,0:T(8,128)S(1)} all-to-all(f32[32,16,128]{2,1,0:T(8,128)S(1)} %broadcast_in_dim.2), channel_id=1, replica_groups=mesh['ta'=8,'gx'=4,'yz'=8] {'gx','yz'}, dimensions={0} | all-to-all | bytes 524288 | tf_op jit(solution)/shard_map/all_to_all | solution.py:111
  72.5 0.7 copy.9
  (4 shorter events, 0.2 us)
Async XLA Ops:
  1.0 11.7 %collective-permute-start = (bf16[2,3,1,8,32,128]{5,4,3,2,1,0:T(8,128)(2,1)S(1)}, bf16[2,3,1,8,32,128]{5,4,3,2,1,0:T(8,128)(2,1)S(1)}, u32[]{:S(2)}, u32[]{:S(2)}) collective-permute-start(bf16[2,3,1,8,32,128]{5,4,3,2,1,0:T(8,128)(2,1)S(1)} %slice.6), channel_id=1, source_target_pairs={{0,24},{8,0},{16,8},{24,16},{1,25},{9,1},{17,9},{25,17},{2,26},{10... | collective-permute-start | bytes 1179656 | tf_op jit(solution)/shard_map/ppermute | solution.py:14
  5.4 10.0 %collective-permute-start.1 = (bf16[2,3,8,1,32,128]{5,4,3,2,1,0:T(8,128)(2,1)S(1)}, bf16[2,3,8,1,32,128]{5,4,3,2,1,0:T(8,128)(2,1)S(1)}, u32[]{:S(2)}, u32[]{:S(2)}) collective-permute-start(bf16[2,3,8,1,32,128]{5,4,3,2,1,0:T(8,128)(2,1)S(1)} %slice.7), channel_id=1, source_target_pairs={{0,7},{1,0},{2,1},{3,2},{4,3},{5,4},{6,5},{7,6},{8,15},{9,8},{10,9... | collective-permute-start | bytes 1179656 | tf_op jit(solution)/shard_map/ppermute | solution.py:14
  12.7 2.7 %copy-start = (bf16[2,3,1,8,32,128]{5,4,3,2,1,0:T(8,128)(2,1)}, bf16[2,3,1,8,32,128]{5,4,3,2,1,0:T(8,128)(2,1)S(1)}, u32[]{:S(2)}) copy-start(bf16[2,3,1,8,32,128]{5,4,3,2,1,0:T(8,128)(2,1)S(1)} %collective-permute-done.refs_1_) | copy-start | bytes 1179652
  15.4 0.7 %copy-start.1 = (bf16[2,3,8,1,32,128]{5,4,3,2,1,0:T(8,128)(2,1)}, bf16[2,3,8,1,32,128]{5,4,3,2,1,0:T(8,128)(2,1)S(1)}, u32[]{:S(2)}) copy-start(bf16[2,3,8,1,32,128]{5,4,3,2,1,0:T(8,128)(2,1)S(1)} %collective-permute-done.1.refs_2_) | copy-start | bytes 1179652

commit v4 on v3

--- a/solution.py
+++ b/solution.py
@@ -14,16 +14,20 @@
     return lax.ppermute(value, axis, pairs)
 
 
-def elementals_kernel(scaling, v_ref, hx_ref, hy_ref, g_ref, o_ref, vt_ref, wy_ref, r_ref, acc_a, acc_b):
+def elementals_kernel(scaling, v_ref, hx_ref, hy_ref, g_ref, o_ref, vt_ref, wy_ref, r_ref):
     planes, lines, row, vecs = v_ref.shape[2:]
     sites = lines * row
+    span = 3 * sites
     step = 16
     nt = (((1,), (1,)), ((), ()))
+
+    def lanes(p, a):
+        return pl.ds(pl.multiple_of(p * span + a * sites, sites), sites)
 
     def transpose_plane(p, carry):
         for c in range(2):
             for a in range(3):
-                vt_ref[c, a, p] = v_ref[c, a, p].reshape(sites, vecs).T
+                vt_ref[c, :, lanes(p, a)] = v_ref[c, a, p].reshape(sites, vecs).T
                 inner = v_ref[c, a, p, 1:].reshape(sites - row, vecs)
                 wy_ref[c, a, p] = jnp.concatenate([inner, hy_ref[c, a, p, 0]], 0).T
         return carry
@@ -31,15 +35,13 @@
     lax.fori_loop(0, planes, transpose_plane, 0)
     for c in range(2):
         for a in range(3):
-            vt_ref[c, a, planes] = hx_ref[c, a, 0].reshape(sites, vecs).T
-    acc_a[...] = jnp.zeros_like(acc_a)
-    acc_b[...] = jnp.zeros_like(acc_b)
+            vt_ref[c, :, lanes(planes, a)] = hx_ref[c, a, 0].reshape(sites, vecs).T
 
     def plane(p, carry):
         def rows_block(jc, inner_carry):
             j0 = pl.multiple_of(jc * step, step)
             sources = (
-                lambda c, b: vt_ref[c, b, p + 1, pl.ds(j0, step), :],
+                lambda c, b: vt_ref[c, pl.ds(j0, step), lanes(p + 1, b)],
                 lambda c, b: wy_ref[c, b, p, pl.ds(j0, step), :],
             )
             for d in range(2):
@@ -56,20 +58,18 @@
                         t_im = gr * w_im[b] + gi * w_re[b]
                         re = t_re if re is None else re + t_re
                         im = t_im if im is None else im + t_im
-                    r_ref[a, pl.ds(2 * d * vecs + j0, step), :] = re.astype(jnp.bfloat16)
-                    r_ref[a, pl.ds((2 * d + 1) * vecs + j0, step), :] = im.astype(jnp.bfloat16)
+                    r_ref[pl.ds(2 * d * vecs + j0, step), lanes(p, a)] = re.astype(jnp.bfloat16)
+                    r_ref[pl.ds((2 * d + 1) * vecs + j0, step), lanes(p, a)] = im.astype(jnp.bfloat16)
             return inner_carry
 
         lax.fori_loop(0, vecs // step, rows_block, 0)
-        for a in range(3):
-            right = r_ref[a]
-            acc_a[...] += lax.dot_general(vt_ref[0, a, p], right, nt, preferred_element_type=jnp.float32)
-            acc_b[...] += lax.dot_general(vt_ref[1, a, p], right, nt, preferred_element_type=jnp.float32)
         return carry
 
     lax.fori_loop(0, planes, plane, 0)
-    a = acc_a[...]
-    b = acc_b[...]
+    used = planes * span
+    right = r_ref[...]
+    a = lax.dot_general(vt_ref[0, :, 0:used], right, nt, preferred_element_type=jnp.float32)
+    b = lax.dot_general(vt_ref[1, :, 0:used], right, nt, preferred_element_type=jnp.float32)
     for d in range(2):
         o = 2 * d * vecs
         o_ref[d, 0] = (a[:, o : o + vecs] + b[:, o + vecs : o + 2 * vecs]) * scaling
@@ -92,11 +92,9 @@
         in_specs=[pl.BlockSpec(memory_space=vmem)] * 4,
         out_specs=pl.BlockSpec(memory_space=vmem),
         scratch_shapes=[
-            pltpu.VMEM((2, 3, nx + 1, nv, sites), jnp.bfloat16),
+            pltpu.VMEM((2, nv, (nx + 1) * 3 * sites), jnp.bfloat16),
             pltpu.VMEM((2, 3, nx, nv, sites), jnp.bfloat16),
-            pltpu.VMEM((3, 4 * nv, sites), jnp.bfloat16),
-            pltpu.VMEM((nv, 4 * nv), jnp.float32),
-            pltpu.VMEM((nv, 4 * nv), jnp.float32),
+            pltpu.VMEM((4 * nv, nx * 3 * sites), jnp.bfloat16),
         ],
     )(vectors, from_next_x, from_next_y, site_rows(gauge_x, gauge_y))
 

time: 73.6 us -> 72.8 us (0.989)
    pallas_call x1, Pallas kernels: 15.8 us -> 15.1 us  [partials(): pl.pallas_call(lambda *refs: elementals_kernel(scaling, *refs), out_shape...]
where the time goes in v4:
time: 72.8 us; the launch traced here: 72.4 us
  blocking collectives  40.5 us (56%)
  Pallas kernels  15.1 us (21%)
  starting transfers between devices  7.23 us (10%)
  local copies, waits for them, and re-layouts  6.13 us (8%)
  waiting for transfers between devices  2.68 us (4%)
  other arithmetic  0.79 us (1%)
    all_to_all x1, blocking collectives, reduce_partials(): got = lax.all_to_all(chunks, ('gx', 'yz'), 0, 0, tiled=True)  23.6 us
    all_to_all x1, blocking collectives, reduce_partials(): return lax.all_to_all(every, ('gx', 'yz'), 0, 0, tiled=True).reshape(shape)  16.9 us
    pallas_call x1, Pallas kernels, partials(): pl.pallas_call(lambda *refs: elementals_kernel(scaling, *refs), out_shape...  15.1 us
    ppermute x2, starting transfers between devices, shifted(): return lax.ppermute(value, axis, pairs)  7.23 us
    ppermute x2, waiting for transfers between devices, shifted(): return lax.ppermute(value, axis, pairs)  2.68 us
  transfers between devices with their start and end apart: 2, of which 1 were waited for; matrix products, arithmetic and copies ran while one was open for 6% of the time, Pallas kernels for 0%

profile of v4, /device:TPU:1, one launch (start us, length us, event | category | flops | bytes accessed | tf_op | source)
XLA Modules:
  0.0 72.4 jit_solution(16102354583154778392)
XLA Ops:
  0.0 1.0 %slice.6 = bf16[2,3,1,8,32,128]{5,4,3,2,1,0:T(8,128)(2,1)S(1)} slice(bf16[2,3,8,8,32,128]{5,4,3,2,1,0:T(8,128)(2,1)} %refs_0_.1), slice={[0:2], [0:3], [0:1], [0:8], [0:32], [0:128]} | slice | bytes 786432 | tf_op jit(solution)/shard_map/slice | solution.py:113
  1.0 3.3 %collective-permute-start = (bf16[2,3,1,8,32,128]{5,4,3,2,1,0:T(8,128)(2,1)S(1)}, bf16[2,3,1,8,32,128]{5,4,3,2,1,0:T(8,128)(2,1)S(1)}, u32[]{:S(2)}, u32[]{:S(2)}) collective-permute-start(bf16[2,3,1,8,32,128]{5,4,3,2,1,0:T(8,128)(2,1)S(1)} %slice.6), channel_id=1, source_target_pairs={{0,24},{8,0},{16,8},{24,16},{1,25},{9,1},{17,9},{25,17},{2,26},{10... | collective-permute-start | bytes 1179656 | tf_op jit(solution)/shard_map/ppermute | solution.py:14
  4.3 1.0 %slice.7 = bf16[2,3,8,1,32,128]{5,4,3,2,1,0:T(8,128)(2,1)S(1)} slice(bf16[2,3,8,8,32,128]{5,4,3,2,1,0:T(8,128)(2,1)} %refs_0_.1), slice={[0:2], [0:3], [0:8], [0:1], [0:32], [0:128]} | slice | bytes 786432 | tf_op jit(solution)/shard_map/slice | solution.py:114
  5.4 3.9 %collective-permute-start.1 = (bf16[2,3,8,1,32,128]{5,4,3,2,1,0:T(8,128)(2,1)S(1)}, bf16[2,3,8,1,32,128]{5,4,3,2,1,0:T(8,128)(2,1)S(1)}, u32[]{:S(2)}, u32[]{:S(2)}) collective-permute-start(bf16[2,3,8,1,32,128]{5,4,3,2,1,0:T(8,128)(2,1)S(1)} %slice.7), channel_id=1, source_target_pairs={{0,7},{1,0},{2,1},{3,2},{4,3},{5,4},{6,5},{7,6},{8,15},{9,8},{10,9... | collective-permute-start | bytes 1179656 | tf_op jit(solution)/shard_map/ppermute | solution.py:14
  9.3 1.3 %reshape.14 = f32[18,8,256]{2,1,0:T(8,128)S(1)} reshape(f32[2,3,3,8,8,32]{5,4,3,2,1,0:T(8,128)} %param.5) | data formatting | bytes 294912 | tf_op jit(solution)/shard_map/reshape | solution.py:81
  10.6 1.3 %reshape.13 = f32[18,8,256]{2,1,0:T(8,128)S(1)} reshape(f32[2,3,3,8,8,32]{5,4,3,2,1,0:T(8,128)} %param.4) | data formatting | bytes 294912 | tf_op jit(solution)/shard_map/reshape | solution.py:81
  11.9 0.8 %maximum_bitcast_fusion.refs_3_ = f32[8,36,256]{2,1,0:T(8,128)} fusion(f32[18,8,256]{2,0,1:T(8,128)S(1)} %copy.7, f32[18,8,256]{2,0,1:T(8,128)S(1)} %copy.6), kind=kLoop, calls=%fused_computation | loop fusion | flops 73728 | bytes 589824 | tf_op jit(solution)/shard_map/transpose | solution.py:82
  12.7 0.0 collective-permute-done.refs_1_
  12.7 0.0 copy-start
  12.7 2.7 %collective-permute-done.1.refs_2_ = bf16[2,3,8,1,32,128]{5,4,3,2,1,0:T(8,128)(2,1)S(1)} collective-permute-done((bf16[2,3,8,1,32,128]{5,4,3,2,1,0:T(8,128)(2,1)S(1)}, bf16[2,3,8,1,32,128]{5,4,3,2,1,0:T(8,128)(2,1)S(1)}, u32[]{:S(2)}, u32[]{:S(2)}) %collective-permute-start.1) | collective-permute-done | bytes 393248 | tf_op jit(solution)/shard_map/ppermute | solution.py:14
  15.4 0.0 copy-done
  15.4 0.0 copy-start.1
  15.4 0.7 %copy-done.1 = bf16[2,3,8,1,32,128]{5,4,3,2,1,0:T(8,128)(2,1)} copy-done((bf16[2,3,8,1,32,128]{5,4,3,2,1,0:T(8,128)(2,1)}, bf16[2,3,8,1,32,128]{5,4,3,2,1,0:T(8,128)(2,1)S(1)}, u32[]{:S(2)}) %copy-start.1) | copy-done | bytes 393240
  16.1 15.1 %shard_map.37 = f32[2,2,128,128]{3,2,1,0:T(8,128)} custom-call(bf16[2,3,8,8,32,128]{5,4,3,2,1,0:T(8,128)(2,1)} %refs_0_.1, bf16[2,3,1,8,32,128]{5,4,3,2,1,0:T(8,128)(2,1)} %copy-done, bf16[2,3,8,1,32,128]{5,4,3,2,1,0:T(8,128)(2,1)} %copy-done.1, f32[8,36,256]{2,1,0:T(8,128)} %maximum_bitcast_fusion.refs_3_), custom_call_target="tpu_custom_call" | custom-call | tf_op jit(solution)/shard_map/pallas_call | solution.py:89
  31.2 23.6 %all_to_all.10 = f32[32,16,128]{2,1,0:T(8,128)S(1)} all-to-all(f32[32,16,128]{2,1,0:T(8,128)} %bitcast.8), channel_id=1, replica_groups=mesh['ta'=8,'gx'=4,'yz'=8] {'gx','yz'}, dimensions={0} | all-to-all | bytes 524288 | tf_op jit(solution)/shard_map/all_to_all | solution.py:106
  54.9 16.9 %all_to_all.11 = f32[32,16,128]{2,1,0:T(8,128)S(1)} all-to-all(f32[32,16,128]{2,1,0:T(8,128)S(1)} %broadcast_in_dim.2), channel_id=1, replica_groups=mesh['ta'=8,'gx'=4,'yz'=8] {'gx','yz'}, dimensions={0} | all-to-all | bytes 524288 | tf_op jit(solution)/shard_map/all_to_all | solution.py:109
  71.7 0.7 copy.9
  (4 shorter events, 0.2 us)
Async XLA Ops:
  1.0 11.7 %collective-permute-start = (bf16[2,3,1,8,32,128]{5,4,3,2,1,0:T(8,128)(2,1)S(1)}, bf16[2,3,1,8,32,128]{5,4,3,2,1,0:T(8,128)(2,1)S(1)}, u32[]{:S(2)}, u32[]{:S(2)}) collective-permute-start(bf16[2,3,1,8,32,128]{5,4,3,2,1,0:T(8,128)(2,1)S(1)} %slice.6), channel_id=1, source_target_pairs={{0,24},{8,0},{16,8},{24,16},{1,25},{9,1},{17,9},{25,17},{2,26},{10... | collective-permute-start | bytes 1179656 | tf_op jit(solution)/shard_map/ppermute | solution.py:14
  5.4 10.0 %collective-permute-start.1 = (bf16[2,3,8,1,32,128]{5,4,3,2,1,0:T(8,128)(2,1)S(1)}, bf16[2,3,8,1,32,128]{5,4,3,2,1,0:T(8,128)(2,1)S(1)}, u32[]{:S(2)}, u32[]{:S(2)}) collective-permute-start(bf16[2,3,8,1,32,128]{5,4,3,2,1,0:T(8,128)(2,1)S(1)} %slice.7), channel_id=1, source_target_pairs={{0,7},{1,0},{2,1},{3,2},{4,3},{5,4},{6,5},{7,6},{8,15},{9,8},{10,9... | collective-permute-start | bytes 1179656 | tf_op jit(solution)/shard_map/ppermute | solution.py:14
  12.7 2.7 %copy-start = (bf16[2,3,1,8,32,128]{5,4,3,2,1,0:T(8,128)(2,1)}, bf16[2,3,1,8,32,128]{5,4,3,2,1,0:T(8,128)(2,1)S(1)}, u32[]{:S(2)}) copy-start(bf16[2,3,1,8,32,128]{5,4,3,2,1,0:T(8,128)(2,1)S(1)} %collective-permute-done.refs_1_) | copy-start | bytes 1179652
  15.4 0.7 %copy-start.1 = (bf16[2,3,8,1,32,128]{5,4,3,2,1,0:T(8,128)(2,1)}, bf16[2,3,8,1,32,128]{5,4,3,2,1,0:T(8,128)(2,1)S(1)}, u32[]{:S(2)}) copy-start(bf16[2,3,8,1,32,128]{5,4,3,2,1,0:T(8,128)(2,1)S(1)} %collective-permute-done.1.refs_2_) | copy-start | bytes 1179652

commit v5 on v4

--- a/solution.py
+++ b/solution.py
@@ -14,7 +14,7 @@
     return lax.ppermute(value, axis, pairs)
 
 
-def elementals_kernel(scaling, v_ref, hx_ref, hy_ref, g_ref, o_ref, vt_ref, wy_ref, r_ref):
+def elementals_kernel(scaling, v_ref, hx_ref, g_ref, o_ref, vt_ref, wy_ref, r_ref):
     planes, lines, row, vecs = v_ref.shape[2:]
     sites = lines * row
     span = 3 * sites
@@ -29,7 +29,8 @@
             for a in range(3):
                 vt_ref[c, :, lanes(p, a)] = v_ref[c, a, p].reshape(sites, vecs).T
                 inner = v_ref[c, a, p, 1:].reshape(sites - row, vecs)
-                wy_ref[c, a, p] = jnp.concatenate([inner, hy_ref[c, a, p, 0]], 0).T
+                edge = jnp.zeros((row, vecs), inner.dtype)
+                wy_ref[c, a, p] = jnp.concatenate([inner, edge], 0).T
         return carry
 
     lax.fori_loop(0, planes, transpose_plane, 0)
@@ -86,17 +87,55 @@
     nx, ny, nz, nv = vectors.shape[2:]
     sites = ny * nz
     vmem = pltpu.MemorySpace.VMEM
-    return pl.pallas_call(
+    inner = pl.pallas_call(
         lambda *refs: elementals_kernel(scaling, *refs),
         out_shape=jax.ShapeDtypeStruct((2, 2, nv, nv), jnp.float32),
-        in_specs=[pl.BlockSpec(memory_space=vmem)] * 4,
+        in_specs=[pl.BlockSpec(memory_space=vmem)] * 3,
         out_specs=pl.BlockSpec(memory_space=vmem),
         scratch_shapes=[
             pltpu.VMEM((2, nv, (nx + 1) * 3 * sites), jnp.bfloat16),
             pltpu.VMEM((2, 3, nx, nv, sites), jnp.bfloat16),
             pltpu.VMEM((4 * nv, nx * 3 * sites), jnp.bfloat16),
         ],
-    )(vectors, from_next_x, from_next_y, site_rows(gauge_x, gauge_y))
+    )(vectors, from_next_x, site_rows(gauge_x, gauge_y))
+    inner, from_next_y = lax.optimization_barrier((inner, from_next_y))
+    return inner + last_line_term(vectors, from_next_y, gauge_y, scaling)
+
+
+def colour_apply(gauge, source_vectors):
+    real_parts = []
+    imag_parts = []
+    for colour in range(3):
+        real_running = jnp.zeros(source_vectors.shape[2:], jnp.float32)
+        imaginary_running = jnp.zeros(source_vectors.shape[2:], jnp.float32)
+        for inner_product in range(3):
+            left_real = gauge[0, colour, inner_product][..., None]
+            left_imaginary = gauge[1, colour, inner_product][..., None]
+            right_real = source_vectors[0, inner_product].astype(jnp.float32)
+            right_imaginary = source_vectors[1, inner_product].astype(jnp.float32)
+            real_running = real_running + left_real * right_real - left_imaginary * right_imaginary
+            imaginary_running = (
+                imaginary_running + left_real * right_imaginary + left_imaginary * right_real
+            )
+        real_parts.append(real_running)
+        imag_parts.append(imaginary_running)
+    return jnp.stack([jnp.stack(real_parts), jnp.stack(imag_parts)]).astype(jnp.bfloat16)
+
+
+def last_line_term(vectors, from_next_y, gauge_y, scaling):
+    lines = vectors.shape[3]
+    nv = vectors.shape[-1]
+    image = colour_apply(gauge_y[:, :, :, :, lines - 1 :], from_next_y)
+    left = vectors[:, :, :, lines - 1 :].reshape(-1, nv)
+    right_re = image[0].reshape(-1, nv)
+    right_im = image[1].reshape(-1, nv)
+    right = jnp.concatenate(
+        [jnp.concatenate([right_re, right_im], 1), jnp.concatenate([right_im, -right_re], 1)], 0
+    )
+    dims = (((0,), (0,)), ((), ()))
+    both = lax.dot_general(left, right, dims, preferred_element_type=jnp.float32)
+    term = both.reshape(nv, 2, nv).transpose(1, 0, 2) * scaling
+    return jnp.stack([jnp.zeros_like(term), term])
 
 
 def reduce_partials(x):

time: 72.8 us -> 69.9 us (0.960)
  waiting for transfers between devices: 2.68 us -> 0.01 us
  local copies, waits for them, and re-layouts: 6.13 us -> 4.83 us
  other arithmetic: 0.79 us -> 1.72 us
    ppermute x2, waiting for transfers between devices: 2.68 us -> 0.01 us  [shifted(): return lax.ppermute(value, axis, pairs)]
    reshape x2, local copies, waits for them, and re-layouts: 1.31 us -> 0.25 us  [site_rows(): gauge_x.reshape(18, nx, ny * nz)]
    reshape x2, local copies, waits for them, and re-layouts: 1.31 us -> 0.25 us  [site_rows(): gauge_y.reshape(18, nx, ny * nz)]
    another operation x0 -> x4, other arithmetic: none -> 0.86 us
    unnamed x5 -> x9, local copies, waits for them, and re-layouts: 1.44 us -> 1.86 us
  transfers between devices with their start and end apart: 2 -> 2, of which waited for: 1 -> 0; matrix products, arithmetic and copies ran while one was open for 6% -> 4% of each run, Pallas kernels for 0% -> 21%
where the time goes in v5:
time: 69.9 us; the launch traced here: 69.7 us
  blocking collectives  40.4 us (58%)
  Pallas kernels  15 us (21%)
  starting transfers between devices  7.23 us (10%)
  local copies, waits for them, and re-layouts  4.83 us (7%)
  other arithmetic  1.72 us (2%)
    all_to_all x1, blocking collectives, reduce_partials(): got = lax.all_to_all(chunks, ('gx', 'yz'), 0, 0, tiled=True)  23.5 us
    all_to_all x1, blocking collectives, reduce_partials(): return lax.all_to_all(every, ('gx', 'yz'), 0, 0, tiled=True).reshape(shape)  16.9 us
    pallas_call x1, Pallas kernels, partials(): pl.pallas_call(lambda *refs: elementals_kernel(scaling, *refs), out_shape...  15 us
    ppermute x2, starting transfers between devices, shifted(): return lax.ppermute(value, axis, pairs)  7.23 us
    unnamed x9, local copies, waits for them, and re-layouts  1.86 us
  transfers between devices with their start and end apart: 2, of which 0 were waited for; matrix products, arithmetic and copies ran while one was open for 4% of the time, Pallas kernels for 21%

profile of v5, /device:TPU:1, one launch (start us, length us, event | category | flops | bytes accessed | tf_op | source)
XLA Modules:
  0.0 69.7 jit_solution(2383559435591663855)
XLA Ops:
  0.0 1.1 %slice.114 = bf16[2,3,1,8,32,128]{5,4,3,2,1,0:T(8,128)(2,1)S(1)} slice(bf16[2,3,8,8,32,128]{5,4,3,2,1,0:T(8,128)(2,1)} %refs_0_.1), slice={[0:2], [0:3], [0:1], [0:8], [0:32], [0:128]} | slice | bytes 786432 | tf_op jit(solution)/shard_map/slice | solution.py:152
  1.1 3.3 %collective-permute-start = (bf16[2,3,1,8,32,128]{5,4,3,2,1,0:T(8,128)(2,1)S(1)}, bf16[2,3,1,8,32,128]{5,4,3,2,1,0:T(8,128)(2,1)S(1)}, u32[]{:S(2)}, u32[]{:S(2)}) collective-permute-start(bf16[2,3,1,8,32,128]{5,4,3,2,1,0:T(8,128)(2,1)S(1)} %slice.114), channel_id=1, source_target_pairs={{0,24},{8,0},{16,8},{24,16},{1,25},{9,1},{17,9},{25,17},{2,26},{10... | collective-permute-start | bytes 1179656 | tf_op jit(solution)/shard_map/ppermute | solution.py:14
  4.4 1.2 %fusion.44 = (bf16[2,3,8,1,32,128]{5,4,3,2,1,0:T(8,128)(2,1)S(1)}, bf16[2,3,8,1,32,128]{5,4,3,2,1,0:T(8,128)(2,1)S(1)}) fusion(bf16[2,3,8,8,32,128]{5,4,3,2,1,0:T(8,128)(2,1)} %refs_0_.1), kind=kLoop, calls=%fused_computation.91 | loop fusion | bytes 1572864 | tf_op jit(solution)/shard_map/slice | solution.py:129
  5.6 3.9 %collective-permute-start.1 = (bf16[2,3,8,1,32,128]{5,4,3,2,1,0:T(8,128)(2,1)S(1)}, bf16[2,3,8,1,32,128]{5,4,3,2,1,0:T(8,128)(2,1)S(1)}, u32[]{:S(2)}, u32[]{:S(2)}) collective-permute-start(bf16[2,3,8,1,32,128]{5,4,3,2,1,0:T(8,128)(2,1)S(1)} %get-tuple-element.10), channel_id=1, source_target_pairs={{0,7},{1,0},{2,1},{3,2},{4,3},{5,4},{6,5},{7,6},{8,15},{9,8},{10,9... | collective-permute-start | bytes 1179656 | tf_op jit(solution)/shard_map/ppermute | solution.py:14
  9.5 0.0 copy-done.1
  9.5 0.2 reshape.618
  9.8 0.0 copy-done.2
  9.8 0.2 reshape.617
  10.1 0.8 %maximum_bitcast_fusion.refs_2_ = f32[8,36,256]{2,1,0:T(8,128)} fusion(f32[18,8,256]{2,0,1:T(8,128)S(1)} %copy.12, f32[18,8,256]{2,0,1:T(8,128)S(1)} %copy.11), kind=kLoop, calls=%fused_computation.8 | loop fusion | flops 73728 | bytes 589824 | tf_op jit(solution)/shard_map/transpose | solution.py:83
  10.8 0.1 fusion.45
  10.9 0.0 collective-permute-done.refs_1_
  10.9 0.7 %copy-done.3 = bf16[2,3,1,8,32,128]{5,4,3,2,1,0:T(8,128)(2,1)} copy-done((bf16[2,3,1,8,32,128]{5,4,3,2,1,0:T(8,128)(2,1)}, bf16[2,3,1,8,32,128]{5,4,3,2,1,0:T(8,128)(2,1)S(1)}, u32[]{:S(2)}) %copy-start.3) | copy-done | bytes 393240
  11.6 15.0 %shard_map.37 = f32[2,2,128,128]{3,2,1,0:T(8,128)} custom-call(bf16[2,3,8,8,32,128]{5,4,3,2,1,0:T(8,128)(2,1)} %refs_0_.1, bf16[2,3,1,8,32,128]{5,4,3,2,1,0:T(8,128)(2,1)} %copy-done.3, f32[8,36,256]{2,1,0:T(8,128)} %maximum_bitcast_fusion.refs_2_), custom_call_target="tpu_custom_call" | custom-call | tf_op jit(solution)/shard_map/pallas_call | solution.py:90
  26.6 0.0 collective-permute-done.1
  26.6 0.3 fusion.42
  26.9 0.3 fusion.36
  27.2 0.3 fusion.30
  27.6 0.0 copy-start
  27.6 0.4 convolution_multiply_fusion
  28.0 0.1 copy.18
  28.1 0.4 copy-done
  28.5 23.5 %all_to_all.10 = f32[32,16,128]{2,1,0:T(8,128)S(1)} all-to-all(f32[32,16,128]{2,1,0:T(8,128)S(1)} %bitcast.128), channel_id=1, replica_groups=mesh['ta'=8,'gx'=4,'yz'=8] {'gx','yz'}, dimensions={0} | all-to-all | bytes 524288 | tf_op jit(solution)/shard_map/all_to_all | solution.py:145
  52.1 16.9 %all_to_all.11 = f32[32,16,128]{2,1,0:T(8,128)S(1)} all-to-all(f32[32,16,128]{2,1,0:T(8,128)S(1)} %broadcast_in_dim.2), channel_id=1, replica_groups=mesh['ta'=8,'gx'=4,'yz'=8] {'gx','yz'}, dimensions={0} | all-to-all | bytes 524288 | tf_op jit(solution)/shard_map/all_to_all | solution.py:148
  69.0 0.7 %copy.20 = f32[2,2,128,128]{3,2,1,0:T(8,128)} copy(f32[2,2,128,128]{3,2,1,0:T(8,128)S(1)} %bitcast.129) | data formatting | bytes 524288
  (10 shorter events, 0.3 us)
Async XLA Ops:
  0.0 9.5 %copy-start.1 = (f32[2,3,3,8,8,32]{5,4,3,2,1,0:T(8,128)S(1)}, f32[2,3,3,8,8,32]{5,4,3,2,1,0:T(8,128)}, u32[]{:S(2)}) copy-start(f32[2,3,3,8,8,32]{5,4,3,2,1,0:T(8,128)} %param.5) | copy-start | bytes 442372
  0.0 9.8 %copy-start.2 = (f32[2,3,3,8,8,32]{5,4,3,2,1,0:T(8,128)S(1)}, f32[2,3,3,8,8,32]{5,4,3,2,1,0:T(8,128)}, u32[]{:S(2)}) copy-start(f32[2,3,3,8,8,32]{5,4,3,2,1,0:T(8,128)} %param.4) | copy-start | bytes 442372
  1.1 9.8 %collective-permute-start = (bf16[2,3,1,8,32,128]{5,4,3,2,1,0:T(8,128)(2,1)S(1)}, bf16[2,3,1,8,32,128]{5,4,3,2,1,0:T(8,128)(2,1)S(1)}, u32[]{:S(2)}, u32[]{:S(2)}) collective-permute-start(bf16[2,3,1,8,32,128]{5,4,3,2,1,0:T(8,128)(2,1)S(1)} %slice.114), channel_id=1, source_target_pairs={{0,24},{8,0},{16,8},{24,16},{1,25},{9,1},{17,9},{25,17},{2,26},{10... | collective-permute-start | bytes 1179656 | tf_op jit(solution)/shard_map/ppermute | solution.py:14
  5.6 21.0 %collective-permute-start.1 = (bf16[2,3,8,1,32,128]{5,4,3,2,1,0:T(8,128)(2,1)S(1)}, bf16[2,3,8,1,32,128]{5,4,3,2,1,0:T(8,128)(2,1)S(1)}, u32[]{:S(2)}, u32[]{:S(2)}) collective-permute-start(bf16[2,3,8,1,32,128]{5,4,3,2,1,0:T(8,128)(2,1)S(1)} %get-tuple-element.10), channel_id=1, source_target_pairs={{0,7},{1,0},{2,1},{3,2},{4,3},{5,4},{6,5},{7,6},{8,15},{9,8},{10,9... | collective-permute-start | bytes 1179656 | tf_op jit(solution)/shard_map/ppermute | solution.py:14
  10.9 0.7 %copy-start.3 = (bf16[2,3,1,8,32,128]{5,4,3,2,1,0:T(8,128)(2,1)}, bf16[2,3,1,8,32,128]{5,4,3,2,1,0:T(8,128)(2,1)S(1)}, u32[]{:S(2)}) copy-start(bf16[2,3,1,8,32,128]{5,4,3,2,1,0:T(8,128)(2,1)S(1)} %collective-permute-done.refs_1_) | copy-start | bytes 1179652
  27.6 1.0 %copy-start = (f32[2,2,128,128]{3,2,1,0:T(8,128)S(1)}, f32[2,2,128,128]{3,2,1,0:T(8,128)}, u32[]{:S(2)}) copy-start(f32[2,2,128,128]{3,2,1,0:T(8,128)} %shard_map.37) | copy-start | bytes 786436

commit v6 on v5

--- a/solution.py
+++ b/solution.py
@@ -14,7 +14,7 @@
     return lax.ppermute(value, axis, pairs)
 
 
-def elementals_kernel(scaling, v_ref, hx_ref, g_ref, o_ref, vt_ref, wy_ref, r_ref):
+def elementals_kernel(scaling, v_ref, g_ref, o_ref, vt_ref, wy_ref, r_ref):
     planes, lines, row, vecs = v_ref.shape[2:]
     sites = lines * row
     span = 3 * sites
@@ -36,7 +36,7 @@
     lax.fori_loop(0, planes, transpose_plane, 0)
     for c in range(2):
         for a in range(3):
-            vt_ref[c, :, lanes(planes, a)] = hx_ref[c, a, 0].reshape(sites, vecs).T
+            vt_ref[c, :, lanes(planes, a)] = jnp.zeros((vecs, sites), vt_ref.dtype)
 
     def plane(p, carry):
         def rows_block(jc, inner_carry):
@@ -90,16 +90,22 @@
     inner = pl.pallas_call(
         lambda *refs: elementals_kernel(scaling, *refs),
         out_shape=jax.ShapeDtypeStruct((2, 2, nv, nv), jnp.float32),
-        in_specs=[pl.BlockSpec(memory_space=vmem)] * 3,
+        in_specs=[pl.BlockSpec(memory_space=vmem)] * 2,
         out_specs=pl.BlockSpec(memory_space=vmem),
         scratch_shapes=[
             pltpu.VMEM((2, nv, (nx + 1) * 3 * sites), jnp.bfloat16),
             pltpu.VMEM((2, 3, nx, nv, sites), jnp.bfloat16),
             pltpu.VMEM((4 * nv, nx * 3 * sites), jnp.bfloat16),
         ],
-    )(vectors, from_next_x, site_rows(gauge_x, gauge_y))
-    inner, from_next_y = lax.optimization_barrier((inner, from_next_y))
-    return inner + last_line_term(vectors, from_next_y, gauge_y, scaling)
+    )(vectors, site_rows(gauge_x, gauge_y))
+    inner, from_next_x, from_next_y = lax.optimization_barrier((inner, from_next_x, from_next_y))
+    edges = jnp.stack(
+        [
+            last_term(vectors[:, :, nx - 1 :], from_next_x, gauge_x[:, :, :, nx - 1 :], scaling),
+            last_term(vectors[:, :, :, ny - 1 :], from_next_y, gauge_y[:, :, :, :, ny - 1 :], scaling),
+        ]
+    )
+    return inner + edges
 
 
 def colour_apply(gauge, source_vectors):
@@ -122,11 +128,10 @@
     return jnp.stack([jnp.stack(real_parts), jnp.stack(imag_parts)]).astype(jnp.bfloat16)
 
 
-def last_line_term(vectors, from_next_y, gauge_y, scaling):
-    lines = vectors.shape[3]
-    nv = vectors.shape[-1]
-    image = colour_apply(gauge_y[:, :, :, :, lines - 1 :], from_next_y)
-    left = vectors[:, :, :, lines - 1 :].reshape(-1, nv)
+def last_term(left_vectors, source, gauge, scaling):
+    nv = left_vectors.shape[-1]
+    image = colour_apply(gauge, source)
+    left = left_vectors.reshape(-1, nv)
     right_re = image[0].reshape(-1, nv)
     right_im = image[1].reshape(-1, nv)
     right = jnp.concatenate(
@@ -134,8 +139,7 @@
     )
     dims = (((0,), (0,)), ((), ()))
     both = lax.dot_general(left, right, dims, preferred_element_type=jnp.float32)
-    term = both.reshape(nv, 2, nv).transpose(1, 0, 2) * scaling
-    return jnp.stack([jnp.zeros_like(term), term])
+    return both.reshape(nv, 2, nv).transpose(1, 0, 2) * scaling
 
 
 def reduce_partials(x):

time: 69.9 us -> 66.4 us (0.950)
  blocking collectives: 40.4 us -> 35.5 us
  other arithmetic: 1.72 us -> 2.62 us
    all_to_all x1, blocking collectives: 23.5 us -> 18.6 us  [reduce_partials(): got = lax.all_to_all(chunks, ('gx', 'yz'), 0, 0, tiled=True)]
    slice x2, local copies, waits for them, and re-layouts: 2.29 us -> 3.14 us  [the longest x1 1.91 us: partials(): vectors[:, :, :, ny - 1:]]
    another operation x3 -> x6, other arithmetic: 0.81 us -> 1.63 us
    unnamed x9 -> x7, local copies, waits for them, and re-layouts: 1.86 us -> 1.14 us
  transfers between devices with their start and end apart: 2 -> 2, of which waited for: 0 -> 0; matrix products, arithmetic and copies ran while one was open for 4% -> 5% of each run, Pallas kernels for 21% -> 22%
where the time goes in v6:
time: 66.4 us; the launch traced here: 66.1 us
  blocking collectives  35.5 us (53%)
  Pallas kernels  14.8 us (22%)
  starting transfers between devices  7.16 us (11%)
  local copies, waits for them, and re-layouts  5.06 us (8%)
  other arithmetic  2.62 us (4%)
  matrix products  0.83 us (1%)
    all_to_all x1, blocking collectives, reduce_partials(): got = lax.all_to_all(chunks, ('gx', 'yz'), 0, 0, tiled=True)  18.6 us
    all_to_all x1, blocking collectives, reduce_partials(): return lax.all_to_all(every, ('gx', 'yz'), 0, 0, tiled=True).reshape(shape)  16.9 us
    pallas_call x1, Pallas kernels, partials(): pl.pallas_call(lambda *refs: elementals_kernel(scaling, *refs), out_shape...  14.8 us
    ppermute x2, starting transfers between devices, shifted(): return lax.ppermute(value, axis, pairs)  7.16 us
    slice x1, local copies, waits for them, and re-layouts, partials(): vectors[:, :, :, ny - 1:]  1.91 us
    another operation x6, other arithmetic  1.63 us
  transfers between devices with their start and end apart: 2, of which 0 were waited for; matrix products, arithmetic and copies ran while one was open for 5% of the time, Pallas kernels for 22%

profile of v6, /device:TPU:1, one launch (start us, length us, event | category | flops | bytes accessed | tf_op | source)
XLA Modules:
  0.0 66.1 jit_solution(13504513832207546837)
XLA Ops:
  0.0 1.2 %fusion.88 = (bf16[2,3,1,8,32,128]{5,4,3,2,1,0:T(8,128)(2,1)S(1)}, bf16[2,3,1,8,32,128]{5,4,3,2,1,0:T(8,128)(2,1)S(1)}) fusion(bf16[2,3,8,8,32,128]{5,4,3,2,1,0:T(8,128)(2,1)} %refs_0_.1), kind=kLoop, calls=%fused_computation.193 | loop fusion | bytes 1572864 | tf_op jit(solution)/shard_map/slice | solution.py:104
  1.2 3.3 %collective-permute-start = (bf16[2,3,1,8,32,128]{5,4,3,2,1,0:T(8,128)(2,1)S(1)}, bf16[2,3,1,8,32,128]{5,4,3,2,1,0:T(8,128)(2,1)S(1)}, u32[]{:S(2)}, u32[]{:S(2)}) collective-permute-start(bf16[2,3,1,8,32,128]{5,4,3,2,1,0:T(8,128)(2,1)S(1)} %get-tuple-element.12), channel_id=1, source_target_pairs={{0,24},{8,0},{16,8},{24,16},{1,25},{9,1},{17,9},{25,17},{2,26},{10... | collective-permute-start | bytes 1179656 | tf_op jit(solution)/shard_map/ppermute | solution.py:14
  4.6 1.9 %fusion.89 = (bf16[2,3,8,1,32,128]{5,4,3,2,1,0:T(8,128)(2,1)S(1)}, bf16[2,3,8,1,32,128]{5,4,3,2,1,0:T(8,128)(2,1)}) fusion(bf16[2,3,8,8,32,128]{5,4,3,2,1,0:T(8,128)(2,1)} %refs_0_.1), kind=kLoop, calls=%fused_computation.194 | loop fusion | bytes 1572864 | tf_op jit(solution)/shard_map/slice | solution.py:105
  6.5 3.8 %collective-permute-start.1 = (bf16[2,3,8,1,32,128]{5,4,3,2,1,0:T(8,128)(2,1)}, bf16[2,3,8,1,32,128]{5,4,3,2,1,0:T(8,128)(2,1)S(1)}, u32[]{:S(2)}, u32[]{:S(2)}) collective-permute-start(bf16[2,3,8,1,32,128]{5,4,3,2,1,0:T(8,128)(2,1)} %get-tuple-element.14), channel_id=1, source_target_pairs={{0,7},{1,0},{2,1},{3,2},{4,3},{5,4},{6,5},{7,6},{8,15},{9,8},{10,9... | collective-permute-start | bytes 1179656 | tf_op jit(solution)/shard_map/ppermute | solution.py:14
  10.3 0.2 reshape.1222
  10.6 0.2 reshape.1221
  10.8 0.8 %maximum_bitcast_fusion.refs_1_ = f32[8,36,256]{2,1,0:T(8,128)} fusion(f32[18,8,256]{2,0,1:T(8,128)S(1)} %copy.12, f32[18,8,256]{2,0,1:T(8,128)S(1)} %copy.11), kind=kLoop, calls=%fused_computation.16 | loop fusion | flops 73728 | bytes 589824 | tf_op jit(solution)/shard_map/transpose | solution.py:83
  11.6 14.8 %shard_map.37 = f32[2,2,128,128]{3,2,1,0:T(8,128)} custom-call(bf16[2,3,8,8,32,128]{5,4,3,2,1,0:T(8,128)(2,1)} %refs_0_.1, f32[8,36,256]{2,1,0:T(8,128)} %maximum_bitcast_fusion.refs_1_), custom_call_target="tpu_custom_call" | custom-call | tf_op jit(solution)/shard_map/pallas_call | solution.py:90
  26.4 0.1 fusion.90
  26.5 0.3 fusion.85
  26.8 0.3 fusion.79
  27.0 0.3 fusion.73
  27.4 0.4 convolution_multiply_fusion
  27.8 0.1 copy.19
  27.9 0.3 fusion.49
  28.2 0.3 fusion.43
  28.5 0.3 fusion.37
  28.9 0.0 copy-start
  28.9 0.4 convolution_multiply_fusion.1
  29.3 0.1 copy.13
  29.4 0.4 copy-done
  29.9 18.6 %all_to_all.10 = f32[32,16,128]{2,1,0:T(8,128)S(1)} all-to-all(f32[32,16,128]{2,1,0:T(8,128)S(1)} %bitcast.223), channel_id=1, replica_groups=mesh['ta'=8,'gx'=4,'yz'=8] {'gx','yz'}, dimensions={0} | all-to-all | bytes 524288 | tf_op jit(solution)/shard_map/all_to_all | solution.py:149
  48.6 16.9 %all_to_all.11 = f32[32,16,128]{2,1,0:T(8,128)S(1)} all-to-all(f32[32,16,128]{2,1,0:T(8,128)S(1)} %broadcast_in_dim.2), channel_id=1, replica_groups=mesh['ta'=8,'gx'=4,'yz'=8] {'gx','yz'}, dimensions={0} | all-to-all | bytes 524288 | tf_op jit(solution)/shard_map/all_to_all | solution.py:152
  65.4 0.7 %copy.21 = f32[2,2,128,128]{3,2,1,0:T(8,128)} copy(f32[2,2,128,128]{3,2,1,0:T(8,128)S(1)} %bitcast.224) | data formatting | bytes 524288
  (16 shorter events, 0.4 us)
Async XLA Ops:
  0.0 10.3 %copy-start.2 = (f32[2,3,3,8,8,32]{5,4,3,2,1,0:T(8,128)S(1)}, f32[2,3,3,8,8,32]{5,4,3,2,1,0:T(8,128)}, u32[]{:S(2)}) copy-start(f32[2,3,3,8,8,32]{5,4,3,2,1,0:T(8,128)} %param.5) | copy-start | bytes 442372
  1.2 9.3 %copy-start.1 = (f32[2,3,3,8,8,32]{5,4,3,2,1,0:T(8,128)S(1)}, f32[2,3,3,8,8,32]{5,4,3,2,1,0:T(8,128)}, u32[]{:S(2)}) copy-start(f32[2,3,3,8,8,32]{5,4,3,2,1,0:T(8,128)} %param.4) | copy-start | bytes 442372
  1.2 25.2 %collective-permute-start = (bf16[2,3,1,8,32,128]{5,4,3,2,1,0:T(8,128)(2,1)S(1)}, bf16[2,3,1,8,32,128]{5,4,3,2,1,0:T(8,128)(2,1)S(1)}, u32[]{:S(2)}, u32[]{:S(2)}) collective-permute-start(bf16[2,3,1,8,32,128]{5,4,3,2,1,0:T(8,128)(2,1)S(1)} %get-tuple-element.12), channel_id=1, source_target_pairs={{0,24},{8,0},{16,8},{24,16},{1,25},{9,1},{17,9},{25,17},{2,26},{10... | collective-permute-start | bytes 1179656 | tf_op jit(solution)/shard_map/ppermute | solution.py:14
  6.5 20.0 %collective-permute-start.1 = (bf16[2,3,8,1,32,128]{5,4,3,2,1,0:T(8,128)(2,1)}, bf16[2,3,8,1,32,128]{5,4,3,2,1,0:T(8,128)(2,1)S(1)}, u32[]{:S(2)}, u32[]{:S(2)}) collective-permute-start(bf16[2,3,8,1,32,128]{5,4,3,2,1,0:T(8,128)(2,1)} %get-tuple-element.14), channel_id=1, source_target_pairs={{0,7},{1,0},{2,1},{3,2},{4,3},{5,4},{6,5},{7,6},{8,15},{9,8},{10,9... | collective-permute-start | bytes 1179656 | tf_op jit(solution)/shard_map/ppermute | solution.py:14
  28.9 1.0 %copy-start = (f32[2,2,128,128]{3,2,1,0:T(8,128)S(1)}, f32[2,2,128,128]{3,2,1,0:T(8,128)}, u32[]{:S(2)}) copy-start(f32[2,2,128,128]{3,2,1,0:T(8,128)} %shard_map.37) | copy-start | bytes 786436

commit v7 on v6

--- a/solution.py
+++ b/solution.py
@@ -68,13 +68,14 @@
 
     lax.fori_loop(0, planes, plane, 0)
     used = planes * span
-    right = r_ref[...]
-    a = lax.dot_general(vt_ref[0, :, 0:used], right, nt, preferred_element_type=jnp.float32)
-    b = lax.dot_general(vt_ref[1, :, 0:used], right, nt, preferred_element_type=jnp.float32)
+    stacked = vt_ref[:, :, 0:used].reshape(2 * vecs, used)
+    both = lax.dot_general(r_ref[...], stacked, nt, preferred_element_type=jnp.float32)
     for d in range(2):
         o = 2 * d * vecs
-        o_ref[d, 0] = (a[:, o : o + vecs] + b[:, o + vecs : o + 2 * vecs]) * scaling
-        o_ref[d, 1] = (a[:, o + vecs : o + 2 * vecs] - b[:, o : o + vecs]) * scaling
+        real = both[o : o + vecs, 0:vecs] + both[o + vecs : o + 2 * vecs, vecs : 2 * vecs]
+        imag = both[o + vecs : o + 2 * vecs, 0:vecs] - both[o : o + vecs, vecs : 2 * vecs]
+        o_ref[d, 0] = real.T * scaling
+        o_ref[d, 1] = imag.T * scaling
 
 
 def site_rows(gauge_x, gauge_y):

time: 66.4 us -> 64.1 us (0.965)
  Pallas kernels: 14.8 us -> 12.5 us
    pallas_call x1, Pallas kernels: 14.8 us -> 12.5 us  [partials(): pl.pallas_call(lambda *refs: elementals_kernel(scaling, *refs), out_shape...]
  transfers between devices with their start and end apart: 2 -> 2, of which waited for: 0 -> 0; matrix products, arithmetic and copies ran while one was open for 5% -> 5% of each run, Pallas kernels for 22% -> 20%
where the time goes in v7:
time: 64.1 us; the launch traced here: 63.9 us
  blocking collectives  35.5 us (55%)
  Pallas kernels  12.5 us (20%)
  starting transfers between devices  7.16 us (11%)
  local copies, waits for them, and re-layouts  5.06 us (8%)
  other arithmetic  2.62 us (4%)
  matrix products  0.82 us (1%)
    all_to_all x1, blocking collectives, reduce_partials(): got = lax.all_to_all(chunks, ('gx', 'yz'), 0, 0, tiled=True)  18.6 us
    all_to_all x1, blocking collectives, reduce_partials(): return lax.all_to_all(every, ('gx', 'yz'), 0, 0, tiled=True).reshape(shape)  16.9 us
    pallas_call x1, Pallas kernels, partials(): pl.pallas_call(lambda *refs: elementals_kernel(scaling, *refs), out_shape...  12.5 us
    ppermute x2, starting transfers between devices, shifted(): return lax.ppermute(value, axis, pairs)  7.16 us
    slice x1, local copies, waits for them, and re-layouts, partials(): vectors[:, :, :, ny - 1:]  1.91 us
    another operation x6, other arithmetic  1.63 us
  transfers between devices with their start and end apart: 2, of which 0 were waited for; matrix products, arithmetic and copies ran while one was open for 5% of the time, Pallas kernels for 20%

profile of v7, /device:TPU:1, one launch (start us, length us, event | category | flops | bytes accessed | tf_op | source)
XLA Modules:
  0.0 63.9 jit_solution(11585958382446202223)
XLA Ops:
  0.0 1.2 %fusion.88 = (bf16[2,3,1,8,32,128]{5,4,3,2,1,0:T(8,128)(2,1)S(1)}, bf16[2,3,1,8,32,128]{5,4,3,2,1,0:T(8,128)(2,1)S(1)}) fusion(bf16[2,3,8,8,32,128]{5,4,3,2,1,0:T(8,128)(2,1)} %refs_0_.1), kind=kLoop, calls=%fused_computation.193 | loop fusion | bytes 1572864 | tf_op jit(solution)/shard_map/slice | solution.py:105
  1.2 3.3 %collective-permute-start = (bf16[2,3,1,8,32,128]{5,4,3,2,1,0:T(8,128)(2,1)S(1)}, bf16[2,3,1,8,32,128]{5,4,3,2,1,0:T(8,128)(2,1)S(1)}, u32[]{:S(2)}, u32[]{:S(2)}) collective-permute-start(bf16[2,3,1,8,32,128]{5,4,3,2,1,0:T(8,128)(2,1)S(1)} %get-tuple-element.12), channel_id=1, source_target_pairs={{0,24},{8,0},{16,8},{24,16},{1,25},{9,1},{17,9},{25,17},{2,26},{10... | collective-permute-start | bytes 1179656 | tf_op jit(solution)/shard_map/ppermute | solution.py:14
  4.6 1.9 %fusion.89 = (bf16[2,3,8,1,32,128]{5,4,3,2,1,0:T(8,128)(2,1)S(1)}, bf16[2,3,8,1,32,128]{5,4,3,2,1,0:T(8,128)(2,1)}) fusion(bf16[2,3,8,8,32,128]{5,4,3,2,1,0:T(8,128)(2,1)} %refs_0_.1), kind=kLoop, calls=%fused_computation.194 | loop fusion | bytes 1572864 | tf_op jit(solution)/shard_map/slice | solution.py:106
  6.5 3.8 %collective-permute-start.1 = (bf16[2,3,8,1,32,128]{5,4,3,2,1,0:T(8,128)(2,1)}, bf16[2,3,8,1,32,128]{5,4,3,2,1,0:T(8,128)(2,1)S(1)}, u32[]{:S(2)}, u32[]{:S(2)}) collective-permute-start(bf16[2,3,8,1,32,128]{5,4,3,2,1,0:T(8,128)(2,1)} %get-tuple-element.14), channel_id=1, source_target_pairs={{0,7},{1,0},{2,1},{3,2},{4,3},{5,4},{6,5},{7,6},{8,15},{9,8},{10,9... | collective-permute-start | bytes 1179656 | tf_op jit(solution)/shard_map/ppermute | solution.py:14
  10.3 0.2 reshape.1222
  10.6 0.2 reshape.1221
  10.8 0.8 %maximum_bitcast_fusion.refs_1_ = f32[8,36,256]{2,1,0:T(8,128)} fusion(f32[18,8,256]{2,0,1:T(8,128)S(1)} %copy.12, f32[18,8,256]{2,0,1:T(8,128)S(1)} %copy.11), kind=kLoop, calls=%fused_computation.16 | loop fusion | flops 73728 | bytes 589824 | tf_op jit(solution)/shard_map/transpose | solution.py:84
  11.6 12.5 %shard_map.37 = f32[2,2,128,128]{3,2,1,0:T(8,128)} custom-call(bf16[2,3,8,8,32,128]{5,4,3,2,1,0:T(8,128)(2,1)} %refs_0_.1, f32[8,36,256]{2,1,0:T(8,128)} %maximum_bitcast_fusion.refs_1_), custom_call_target="tpu_custom_call" | custom-call | tf_op jit(solution)/shard_map/pallas_call | solution.py:91
  24.1 0.1 fusion.90
  24.2 0.3 fusion.85
  24.5 0.3 fusion.79
  24.8 0.3 fusion.73
  25.2 0.4 convolution_multiply_fusion
  25.6 0.1 copy.19
  25.7 0.3 fusion.49
  26.0 0.3 fusion.43
  26.2 0.3 fusion.37
  26.6 0.0 copy-start
  26.6 0.4 convolution_multiply_fusion.1
  27.0 0.1 copy.13
  27.2 0.4 copy-done
  27.6 18.6 %all_to_all.10 = f32[32,16,128]{2,1,0:T(8,128)S(1)} all-to-all(f32[32,16,128]{2,1,0:T(8,128)S(1)} %bitcast.223), channel_id=1, replica_groups=mesh['ta'=8,'gx'=4,'yz'=8] {'gx','yz'}, dimensions={0} | all-to-all | bytes 524288 | tf_op jit(solution)/shard_map/all_to_all | solution.py:150
  46.3 16.9 %all_to_all.11 = f32[32,16,128]{2,1,0:T(8,128)S(1)} all-to-all(f32[32,16,128]{2,1,0:T(8,128)S(1)} %broadcast_in_dim.2), channel_id=1, replica_groups=mesh['ta'=8,'gx'=4,'yz'=8] {'gx','yz'}, dimensions={0} | all-to-all | bytes 524288 | tf_op jit(solution)/shard_map/all_to_all | solution.py:153
  63.2 0.7 %copy.21 = f32[2,2,128,128]{3,2,1,0:T(8,128)} copy(f32[2,2,128,128]{3,2,1,0:T(8,128)S(1)} %bitcast.224) | data formatting | bytes 524288
  (16 shorter events, 0.4 us)
Async XLA Ops:
  0.0 10.3 %copy-start.2 = (f32[2,3,3,8,8,32]{5,4,3,2,1,0:T(8,128)S(1)}, f32[2,3,3,8,8,32]{5,4,3,2,1,0:T(8,128)}, u32[]{:S(2)}) copy-start(f32[2,3,3,8,8,32]{5,4,3,2,1,0:T(8,128)} %param.5) | copy-start | bytes 442372
  1.2 9.3 %copy-start.1 = (f32[2,3,3,8,8,32]{5,4,3,2,1,0:T(8,128)S(1)}, f32[2,3,3,8,8,32]{5,4,3,2,1,0:T(8,128)}, u32[]{:S(2)}) copy-start(f32[2,3,3,8,8,32]{5,4,3,2,1,0:T(8,128)} %param.4) | copy-start | bytes 442372
  1.2 22.9 %collective-permute-start = (bf16[2,3,1,8,32,128]{5,4,3,2,1,0:T(8,128)(2,1)S(1)}, bf16[2,3,1,8,32,128]{5,4,3,2,1,0:T(8,128)(2,1)S(1)}, u32[]{:S(2)}, u32[]{:S(2)}) collective-permute-start(bf16[2,3,1,8,32,128]{5,4,3,2,1,0:T(8,128)(2,1)S(1)} %get-tuple-element.12), channel_id=1, source_target_pairs={{0,24},{8,0},{16,8},{24,16},{1,25},{9,1},{17,9},{25,17},{2,26},{10... | collective-permute-start | bytes 1179656 | tf_op jit(solution)/shard_map/ppermute | solution.py:14
  6.5 17.7 %collective-permute-start.1 = (bf16[2,3,8,1,32,128]{5,4,3,2,1,0:T(8,128)(2,1)}, bf16[2,3,8,1,32,128]{5,4,3,2,1,0:T(8,128)(2,1)S(1)}, u32[]{:S(2)}, u32[]{:S(2)}) collective-permute-start(bf16[2,3,8,1,32,128]{5,4,3,2,1,0:T(8,128)(2,1)} %get-tuple-element.14), channel_id=1, source_target_pairs={{0,7},{1,0},{2,1},{3,2},{4,3},{5,4},{6,5},{7,6},{8,15},{9,8},{10,9... | collective-permute-start | bytes 1179656 | tf_op jit(solution)/shard_map/ppermute | solution.py:14
  26.6 1.0 %copy-start = (f32[2,2,128,128]{3,2,1,0:T(8,128)S(1)}, f32[2,2,128,128]{3,2,1,0:T(8,128)}, u32[]{:S(2)}) copy-start(f32[2,2,128,128]{3,2,1,0:T(8,128)} %shard_map.37) | copy-start | bytes 786436

commit v8 on v7

--- a/solution.py
+++ b/solution.py
@@ -33,7 +33,7 @@
                 wy_ref[c, a, p] = jnp.concatenate([inner, edge], 0).T
         return carry
 
-    lax.fori_loop(0, planes, transpose_plane, 0)
+    lax.fori_loop(0, planes, transpose_plane, 0, unroll=2)
     for c in range(2):
         for a in range(3):
             vt_ref[c, :, lanes(planes, a)] = jnp.zeros((vecs, sites), vt_ref.dtype)
@@ -63,7 +63,7 @@
                     r_ref[pl.ds((2 * d + 1) * vecs + j0, step), lanes(p, a)] = im.astype(jnp.bfloat16)
             return inner_carry
 
-        lax.fori_loop(0, vecs // step, rows_block, 0)
+        lax.fori_loop(0, vecs // step, rows_block, 0, unroll=2)
         return carry
 
     lax.fori_loop(0, planes, plane, 0)

time: 64.1 us -> 63.8 us (level)
  transfers between devices with their start and end apart: 2 -> 2, of which waited for: 0 -> 0; matrix products, arithmetic and copies ran while one was open for 5% -> 5% of each run, Pallas kernels for 20% -> 19%
where the time goes in v8:
time: 63.8 us; the launch traced here: 63.6 us
  blocking collectives  35.5 us (56%)
  Pallas kernels  12.2 us (19%)
  starting transfers between devices  7.16 us (11%)
  local copies, waits for them, and re-layouts  5.06 us (8%)
  other arithmetic  2.62 us (4%)
  matrix products  0.83 us (1%)
    all_to_all x1, blocking collectives, reduce_partials(): got = lax.all_to_all(chunks, ('gx', 'yz'), 0, 0, tiled=True)  18.6 us
    all_to_all x1, blocking collectives, reduce_partials(): return lax.all_to_all(every, ('gx', 'yz'), 0, 0, tiled=True).reshape(shape)  16.9 us
    pallas_call x1, Pallas kernels, partials(): pl.pallas_call(lambda *refs: elementals_kernel(scaling, *refs), out_shape...  12.2 us
    ppermute x2, starting transfers between devices, shifted(): return lax.ppermute(value, axis, pairs)  7.16 us
    slice x1, local copies, waits for them, and re-layouts, partials(): vectors[:, :, :, ny - 1:]  1.91 us
    another operation x6, other arithmetic  1.63 us
  transfers between devices with their start and end apart: 2, of which 0 were waited for; matrix products, arithmetic and copies ran while one was open for 5% of the time, Pallas kernels for 19%

profile of v8, /device:TPU:1, one launch (start us, length us, event | category | flops | bytes accessed | tf_op | source)
XLA Modules:
  0.0 63.6 jit_solution(4931886250470985972)
XLA Ops:
  0.0 1.2 %fusion.88 = (bf16[2,3,1,8,32,128]{5,4,3,2,1,0:T(8,128)(2,1)S(1)}, bf16[2,3,1,8,32,128]{5,4,3,2,1,0:T(8,128)(2,1)S(1)}) fusion(bf16[2,3,8,8,32,128]{5,4,3,2,1,0:T(8,128)(2,1)} %refs_0_.1), kind=kLoop, calls=%fused_computation.193 | loop fusion | bytes 1572864 | tf_op jit(solution)/shard_map/slice | solution.py:105
  1.2 3.3 %collective-permute-start = (bf16[2,3,1,8,32,128]{5,4,3,2,1,0:T(8,128)(2,1)S(1)}, bf16[2,3,1,8,32,128]{5,4,3,2,1,0:T(8,128)(2,1)S(1)}, u32[]{:S(2)}, u32[]{:S(2)}) collective-permute-start(bf16[2,3,1,8,32,128]{5,4,3,2,1,0:T(8,128)(2,1)S(1)} %get-tuple-element.12), channel_id=1, source_target_pairs={{0,24},{8,0},{16,8},{24,16},{1,25},{9,1},{17,9},{25,17},{2,26},{10... | collective-permute-start | bytes 1179656 | tf_op jit(solution)/shard_map/ppermute | solution.py:14
  4.6 1.9 %fusion.89 = (bf16[2,3,8,1,32,128]{5,4,3,2,1,0:T(8,128)(2,1)S(1)}, bf16[2,3,8,1,32,128]{5,4,3,2,1,0:T(8,128)(2,1)}) fusion(bf16[2,3,8,8,32,128]{5,4,3,2,1,0:T(8,128)(2,1)} %refs_0_.1), kind=kLoop, calls=%fused_computation.194 | loop fusion | bytes 1572864 | tf_op jit(solution)/shard_map/slice | solution.py:106
  6.5 3.8 %collective-permute-start.1 = (bf16[2,3,8,1,32,128]{5,4,3,2,1,0:T(8,128)(2,1)}, bf16[2,3,8,1,32,128]{5,4,3,2,1,0:T(8,128)(2,1)S(1)}, u32[]{:S(2)}, u32[]{:S(2)}) collective-permute-start(bf16[2,3,8,1,32,128]{5,4,3,2,1,0:T(8,128)(2,1)} %get-tuple-element.14), channel_id=1, source_target_pairs={{0,7},{1,0},{2,1},{3,2},{4,3},{5,4},{6,5},{7,6},{8,15},{9,8},{10,9... | collective-permute-start | bytes 1179656 | tf_op jit(solution)/shard_map/ppermute | solution.py:14
  10.3 0.2 reshape.1222
  10.6 0.2 reshape.1221
  10.8 0.8 %maximum_bitcast_fusion.refs_1_ = f32[8,36,256]{2,1,0:T(8,128)} fusion(f32[18,8,256]{2,0,1:T(8,128)S(1)} %copy.12, f32[18,8,256]{2,0,1:T(8,128)S(1)} %copy.11), kind=kLoop, calls=%fused_computation.16 | loop fusion | flops 73728 | bytes 589824 | tf_op jit(solution)/shard_map/transpose | solution.py:84
  11.6 12.2 %shard_map.37 = f32[2,2,128,128]{3,2,1,0:T(8,128)} custom-call(bf16[2,3,8,8,32,128]{5,4,3,2,1,0:T(8,128)(2,1)} %refs_0_.1, f32[8,36,256]{2,1,0:T(8,128)} %maximum_bitcast_fusion.refs_1_), custom_call_target="tpu_custom_call" | custom-call | tf_op jit(solution)/shard_map/pallas_call | solution.py:91
  23.9 0.1 fusion.90
  24.0 0.3 fusion.85
  24.2 0.3 fusion.79
  24.5 0.3 fusion.73
  24.9 0.4 convolution_multiply_fusion
  25.3 0.1 copy.19
  25.4 0.3 fusion.49
  25.7 0.3 fusion.43
  26.0 0.3 fusion.37
  26.4 0.0 copy-start
  26.4 0.4 convolution_multiply_fusion.1
  26.8 0.1 copy.13
  26.9 0.4 copy-done
  27.4 18.6 %all_to_all.10 = f32[32,16,128]{2,1,0:T(8,128)S(1)} all-to-all(f32[32,16,128]{2,1,0:T(8,128)S(1)} %bitcast.223), channel_id=1, replica_groups=mesh['ta'=8,'gx'=4,'yz'=8] {'gx','yz'}, dimensions={0} | all-to-all | bytes 524288 | tf_op jit(solution)/shard_map/all_to_all | solution.py:150
  46.0 16.9 %all_to_all.11 = f32[32,16,128]{2,1,0:T(8,128)S(1)} all-to-all(f32[32,16,128]{2,1,0:T(8,128)S(1)} %broadcast_in_dim.2), channel_id=1, replica_groups=mesh['ta'=8,'gx'=4,'yz'=8] {'gx','yz'}, dimensions={0} | all-to-all | bytes 524288 | tf_op jit(solution)/shard_map/all_to_all | solution.py:153
  62.9 0.7 %copy.21 = f32[2,2,128,128]{3,2,1,0:T(8,128)} copy(f32[2,2,128,128]{3,2,1,0:T(8,128)S(1)} %bitcast.224) | data formatting | bytes 524288
  (16 shorter events, 0.4 us)
Async XLA Ops:
  0.0 10.3 %copy-start.2 = (f32[2,3,3,8,8,32]{5,4,3,2,1,0:T(8,128)S(1)}, f32[2,3,3,8,8,32]{5,4,3,2,1,0:T(8,128)}, u32[]{:S(2)}) copy-start(f32[2,3,3,8,8,32]{5,4,3,2,1,0:T(8,128)} %param.5) | copy-start | bytes 442372
  1.2 9.3 %copy-start.1 = (f32[2,3,3,8,8,32]{5,4,3,2,1,0:T(8,128)S(1)}, f32[2,3,3,8,8,32]{5,4,3,2,1,0:T(8,128)}, u32[]{:S(2)}) copy-start(f32[2,3,3,8,8,32]{5,4,3,2,1,0:T(8,128)} %param.4) | copy-start | bytes 442372
  1.2 22.7 %collective-permute-start = (bf16[2,3,1,8,32,128]{5,4,3,2,1,0:T(8,128)(2,1)S(1)}, bf16[2,3,1,8,32,128]{5,4,3,2,1,0:T(8,128)(2,1)S(1)}, u32[]{:S(2)}, u32[]{:S(2)}) collective-permute-start(bf16[2,3,1,8,32,128]{5,4,3,2,1,0:T(8,128)(2,1)S(1)} %get-tuple-element.12), channel_id=1, source_target_pairs={{0,24},{8,0},{16,8},{24,16},{1,25},{9,1},{17,9},{25,17},{2,26},{10... | collective-permute-start | bytes 1179656 | tf_op jit(solution)/shard_map/ppermute | solution.py:14
  6.5 17.5 %collective-permute-start.1 = (bf16[2,3,8,1,32,128]{5,4,3,2,1,0:T(8,128)(2,1)}, bf16[2,3,8,1,32,128]{5,4,3,2,1,0:T(8,128)(2,1)S(1)}, u32[]{:S(2)}, u32[]{:S(2)}) collective-permute-start(bf16[2,3,8,1,32,128]{5,4,3,2,1,0:T(8,128)(2,1)} %get-tuple-element.14), channel_id=1, source_target_pairs={{0,7},{1,0},{2,1},{3,2},{4,3},{5,4},{6,5},{7,6},{8,15},{9,8},{10,9... | collective-permute-start | bytes 1179656 | tf_op jit(solution)/shard_map/ppermute | solution.py:14
  26.4 1.0 %copy-start = (f32[2,2,128,128]{3,2,1,0:T(8,128)S(1)}, f32[2,2,128,128]{3,2,1,0:T(8,128)}, u32[]{:S(2)}) copy-start(f32[2,2,128,128]{3,2,1,0:T(8,128)} %shard_map.37) | copy-start | bytes 786436
